TPU v7x, 256 devices: a whole 4x4x8 slice. The times are simulated.
256 devices in a mesh: seg: 8 (over y, core), sec: 32 (over x, z).
Axes of the slice: x: 4, y: 4, z: 8, core: 2. Of those that a mesh axis runs over, the one named last changes fastest.
Arguments:
- psi_init: float32 [8, 32, 256, 256], P('seg', 'sec'), may hold values from -6 to 6
- boundary_env: float32 [32, 18, 256, 256], P('sec')
- right_env: float32 [8, 32, 18, 256, 256], P('seg', 'sec')
- transfer_blocks: float32 [8, 32, 256, 256], P('seg', 'sec')
- transfer_mix: float32 [8, 18, 18], P('seg')
- hop_left: float32 [8, 32, 256, 256], P('seg', 'sec'), may hold values from -0.75 to 0.75
- hop_right: float32 [8, 32, 256, 256], P('seg', 'sec'), may hold values from -0.75 to 0.75
- block_sizes: int32 [8, 2, 32], P('seg'), may hold values from 64 to 256, as said below
- sources: int32 [8, 32], P('seg'), may hold values from 0 to 31, each once within a row
Outputs:
- state: float32 [8, 32, 256, 256], P('seg', 'sec')
Inputs may be any that keep to these rules, and one draw needn't show every extreme that they name: `sources`: each block number appears once in a segment's list. `block_sizes`: each segment has a block with 256 live rows and one with 256 live columns.
All inputs are finite; a program needn't handle non-finite values.
Results may differ from a plain program's by a relative error of at most 0.0003.
Values sent between devices are 32-bit elements; how exact they have to be, the bound alone decides.
No kernel may reach another device: no remote copies, remote signals or barrier semaphores. Data moves between devices by JAX's collectives and lax.ppermute only.
A program may use at most 128 MiB of HBM per device.

v0:
```python
import jax
import jax.numpy as jnp
from jax import lax
from jax.sharding import PartitionSpec as P
from jax.experimental import pallas as pl
from jax.experimental.pallas import tpu as pltpu

DAV = 2


HIGH = lax.Precision.HIGHEST
EPSILON = 1e-06


def passed_along(value, axis, steps):
    count = lax.axis_size(axis)
    initial, last = (max(0, -steps), min(count, count - steps))
    return lax.ppermute(value, axis, [(source, source + steps) for source in range(initial, last)])


def product(left, right):
    return jnp.matmul(left, right, precision=HIGH)


def sec_total(values):
    count = lax.axis_size("sec")
    spread = jnp.broadcast_to(values[None, :], (count, values.shape[0]))
    return jnp.sum(lax.all_to_all(spread, "sec", 0, 0, tiled=True), axis=0)


def regroup(moving, wanted):
    count = lax.axis_size("sec")
    rows, cols = moving.shape
    pieces = moving.reshape(count, rows // count, cols)
    held = lax.all_to_all(pieces, "sec", 0, 0, tiled=True)
    ordered = jnp.take(held, wanted, axis=0, mode="clip")
    back = lax.all_to_all(ordered, "sec", 0, 0, tiled=True)
    return back.reshape(rows, cols)


def _mix_kernel(mix_ref, source_ref, out_ref):
    channels = source_ref.shape[0]
    for w in range(channels):
        acc = source_ref[0] * mix_ref[0, w]
        for u in range(1, channels):
            acc = acc + source_ref[u] * mix_ref[u, w]
        out_ref[w] = acc


def channel_mix(mix, source, rows=64):
    channels, height, width = source.shape
    return pl.pallas_call(
        _mix_kernel,
        grid=(height // rows,),
        in_specs=[
            pl.BlockSpec(memory_space=pltpu.SMEM),
            pl.BlockSpec((channels, rows, width), lambda i: (0, i, 0)),
        ],
        out_specs=pl.BlockSpec((channels, rows, width), lambda i: (0, i, 0)),
        out_shape=jax.ShapeDtypeStruct(source.shape, source.dtype),
    )(mix, source)


def prefix_scan(own_mix, own_blocks):
    seg = lax.axis_index("seg")
    count = lax.axis_size("seg")
    width = own_blocks.shape[0]
    channels = own_mix.shape[0]
    pad = -(-channels // 8) * 8
    eye_mix = jnp.eye(channels, dtype=jnp.float32)
    eye_blocks = jnp.eye(width, dtype=jnp.float32)
    span_mix, span_blocks = own_mix, own_blocks
    before_mix, before_blocks = eye_mix, eye_blocks
    step = 1
    while step < count:
        packed = jnp.concatenate(
            [span_blocks, jnp.pad(span_mix, ((0, pad - channels), (0, width - channels)))], axis=0
        )
        got = passed_along(packed, "seg", step)
        got_blocks = got[:width]
        got_mix = got[width:width + channels, :channels]
        take = seg >= step
        if step == 1:
            before_mix = jnp.where(take, got_mix, eye_mix)
            before_blocks = jnp.where(take, got_blocks, eye_blocks)
        else:
            before_mix = jnp.where(take, product(got_mix, before_mix), before_mix)
            before_blocks = jnp.where(take, product(got_blocks, before_blocks), before_blocks)
        if step * 2 < count:
            span_mix = jnp.where(take, product(got_mix, span_mix), span_mix)
            span_blocks = jnp.where(take, product(got_blocks, span_blocks), span_blocks)
        step *= 2
    return before_mix, before_blocks


def per_device(
    psi_init,
    boundary_env,
    right_env,
    transfer_blocks,
    transfer_mix,
    hop_left,
    hop_right,
    block_sizes,
    sources,
):
    initial = psi_init[0, 0]
    boundary = boundary_env[0]
    right_side = right_env[0, 0]
    own_blocks = transfer_blocks[0, 0]
    own_mix = transfer_mix[0]
    left_hop = hop_left[0, 0]
    right_hop = hop_right[0, 0]
    all_sizes = block_sizes[0]
    all_sources = sources[0]
    block_width = initial.shape[1]
    sector_count = lax.axis_size("sec")
    me = lax.axis_index("sec")

    places = lax.broadcasted_iota(jnp.int32, (block_width,), 0)
    row_live = (places < all_sizes[0, me]).astype(jnp.float32)
    col_live = (places < all_sizes[1, me]).astype(jnp.float32)
    masking = row_live[:, None] * col_live[None, :]

    first = masking * initial
    first_moved = regroup(product(first, right_hop), all_sources)

    eye_lanes = (places[:, None] == places[None, :]).astype(jnp.float32)
    right_diag = jnp.sum(right_side * eye_lanes, axis=2)
    prefix_mix, prefix_blocks = prefix_scan(own_mix, own_blocks)
    mixed = channel_mix(prefix_mix, boundary)
    half = jnp.einsum("wkl,lj->wkj", mixed, prefix_blocks, precision=HIGH)
    left_env = jnp.einsum("ki,wkj->iwj", prefix_blocks, half, precision=HIGH)
    left_diag = jnp.sum(prefix_blocks[None] * half, axis=1)
    diagonal = jnp.einsum("wi,wj->ij", left_diag, right_diag, precision=HIGH)

    def apply_h(vector, moved):
        inner = jnp.einsum("iwj,jk->iwk", left_env, vector, precision=HIGH)
        local_part = jnp.einsum("iwk,wkl->il", inner, right_side, precision=HIGH)
        return masking * (local_part + product(left_hop, moved))

    def step(vector, image_vec, rayleigh):
        residue = image_vec - rayleigh * vector
        shifted = diagonal - rayleigh
        return vector - residue * shifted / (shifted * shifted + 1.0)

    image = apply_h(first, first_moved)
    sums = sec_total(jnp.stack([jnp.sum(first * first), jnp.sum(first * image)]))
    scale = 1.0 / jnp.sqrt(sums[0] + EPSILON)
    vector = first * scale
    image_vec = image * scale
    rayleigh = sums[1] / (sums[0] + EPSILON)
    for turn_index in range(1, DAV):
        update = step(vector, image_vec, rayleigh)
        moved = regroup(product(update, right_hop), all_sources)
        image = apply_h(update, moved)
        sums = sec_total(jnp.stack([jnp.sum(update * update), jnp.sum(update * image)]))
        scale = 1.0 / jnp.sqrt(sums[0] + EPSILON)
        vector = update * scale
        image_vec = image * scale
        rayleigh = sums[1] / (sums[0] + EPSILON)
    update = step(vector, image_vec, rayleigh)
    total = sec_total(jnp.sum(update * update)[None])[0]
    cells = float(sector_count * block_width * block_width)
    return (update * (jnp.sqrt(jnp.float32(cells)) / jnp.sqrt(total + EPSILON)))[None, None]


def solution(mesh):
    return jax.shard_map(
        per_device,
        mesh=mesh,
        in_specs=(
            P("seg", "sec", None, None),
            P("sec", None, None, None),
            P("seg", "sec", None, None, None),
            P("seg", "sec", None, None),
            P("seg", None, None),
            P("seg", "sec", None, None),
            P("seg", "sec", None, None),
            P("seg", None, None),
            P("seg", None),
        ),
        out_specs=P("seg", "sec", None, None),
        check_vma=False,
    )
```

profile of v0, /device:TPU:16, one launch (start us, length us, event | category | flops | bytes accessed | tf_op | source)
XLA Modules:
  0.0 177.9 jit_solution(5468510463549253543)
XLA Ops:
  1.7 1.9 %collective-permute-start = (f32[280,256]{1,0:T(8,128)S(1)}, f32[280,256]{1,0:T(8,128)S(1)}, u32[]{:S(2)}, u32[]{:S(2)}) collective-permute-start(f32[280,256]{1,0:T(8,128)S(1)} %select_maximum_fusion.2), channel_id=1, source_target_pairs={{0,32},{32,64},{64,96},{96,128},{128,160},{160,192},{192,224},{1,3... | collective-permute-start | bytes 860168 | tf_op jit(solution)/shard_map/ppermute | solution.py:18
  3.7 1.4 constant_dynamic-slice_fusion.1
  6.3 2.2 %fusion.19 = f32[32,8,256]{2,1,0:T(8,128)} fusion(f32[1,1,256,256]{3,2,1,0:T(8,128)} %param.15, f32[1,1,256,256]{3,2,1,0:T(8,128)} %param.9, f32[256]{0:T(256)S(1)} %get-tuple-element.23, f32[256]{0:T(256)S(1)} %get-tuple-element.24), kind=kOutput, calls=%fused_computation.34 | convolution fusion | flops 201457664 | bytes 788480 | tf_op jit(solution)/shard_map/dot_general | solution.py:22
  8.5 11.3 %all-to-all-start = ((f32[32,8,256]{2,1,0:T(8,128)}), f32[32,8,256]{2,1,0:T(8,128)S(1)}, u32[]{:S(2)}, u32[]{:S(2)}) async-start(f32[32,8,256]{2,1,0:T(8,128)} %fusion.19), calls=%async_computation | async-start | bytes 524288 | tf_op jit(solution)/shard_map/all_to_all | solution.py:35
  19.8 1.4 convolution_select_fusion.3
  22.2 3.2 %collective-permute-start.1 = (f32[280,256]{1,0:T(8,128)S(1)}, f32[280,256]{1,0:T(8,128)S(1)}, u32[]{:S(2)}, u32[]{:S(2)}) collective-permute-start(f32[280,256]{1,0:T(8,128)S(1)} %select_maximum_fusion.1), channel_id=1, source_target_pairs={{0,64},{32,96},{64,128},{96,160},{128,192},{160,224},{1,65},{33,97... | collective-permute-start | bytes 860168 | tf_op jit(solution)/shard_map/ppermute | solution.py:18
  26.1 6.1 %all-to-all-done = f32[32,8,256]{2,1,0:T(8,128)S(1)} async-done(((f32[32,8,256]{2,1,0:T(8,128)}), f32[32,8,256]{2,1,0:T(8,128)S(1)}, u32[]{:S(2)}, u32[]{:S(2)}) %all-to-all-start) | async-done | bytes 262176 | tf_op jit(solution)/shard_map/all_to_all | solution.py:35
  33.5 5.8 %all-to-all-start.1 = ((f32[32,8,256]{2,1,0:T(8,128)}), f32[32,8,256]{2,1,0:T(8,128)S(1)}, u32[]{:S(2)}, u32[]{:S(2)}) async-start(f32[32,8,256]{2,1,0:T(8,128)} %gather_fusion), calls=%async_computation.1 | async-start | bytes 524288 | tf_op jit(solution)/shard_map/all_to_all | solution.py:37
  41.7 10.1 %collective-permute-done.2 = f32[280,256]{1,0:T(8,128)S(1)} collective-permute-done((f32[280,256]{1,0:T(8,128)S(1)}, f32[280,256]{1,0:T(8,128)S(1)}, u32[]{:S(2)}, u32[]{:S(2)}) %collective-permute-start.2) | collective-permute-done | bytes 286752 | tf_op jit(solution)/shard_map/ppermute | solution.py:18
  52.6 8.3 %shard_map.91 = f32[18,256,256]{2,1,0:T(8,128)} custom-call(f32[18,18]{1,0:T(8,128)} %convolution_select_fusion.4.mix_ref, f32[18,256,256]{2,1,0:T(8,128)} %bitcast.125), custom_call_target="tpu_custom_call" | custom-call | tf_op jit(solution)/shard_map/pallas_call | solution.py:52
  61.3 6.1 %multiply_reduce_fusion = (f32[18,256]{1,0:T(8,128)S(1)}, f32[18,256,256]{2,1,0:T(8,128)S(1)}) fusion(f32[256,256]{1,0:T(8,128)S(1)} %convolution_select_fusion, f32[18,256,256]{2,1,0:T(8,128)} %shard_map.91), kind=kOutput, calls=%fused_computation.8 | convolution fusion | flops 3626233344 | bytes 9717760 | tf_op jit(solution)/shard_map/wkl,lj->wkj/dot_general | solution.py:132
  67.4 4.7 %fusion.32 = f32[256,18,256]{2,0,1:T(8,128)S(1)} fusion(f32[18,256,256]{2,1,0:T(8,128)S(1)} %get-tuple-element.19, f32[256,256]{1,0:T(8,128)S(1)} %convolution_select_fusion), kind=kOutput, calls=%fused_computation.47 | convolution fusion | flops 3623878656 | bytes 9699328 | tf_op jit(solution)/shard_map/ki,wkj->iwj/dot_general | solution.py:133
  72.1 2.1 %copy-done.1 = f32[256,18,256]{2,0,1:T(8,128)} copy-done((f32[256,18,256]{2,0,1:T(8,128)}, f32[256,18,256]{2,0,1:T(8,128)S(1)}, u32[]{:S(2)}) %copy-start.1) | copy-done | bytes 4718616
  74.2 4.5 %fusion.28 = f32[256,18,256]{2,0,1:T(8,128)S(1)} fusion(f32[256,18,256]{2,0,1:T(8,128)S(1)} %fusion.32, f32[1,1,256,256]{3,2,1,0:T(8,128)S(1)} %copy-done.2, f32[256]{0:T(256)S(1)} %get-tuple-element.23, f32[256]{0:T(256)S(1)} %get-tuple-element.24), kind=kOutput, calls=%fused_computation.43 | convolution fusion | flops 3624009728 | bytes 9701376 | tf_op jit(solution)/shard_map/iwj,jk->iwk/dot_general | solution.py:138
  78.8 4.3 %fusion.9 = f32[256,256]{1,0:T(8,128)S(1)} fusion(f32[256,18,256]{2,0,1:T(8,128)S(1)} %fusion.28, f32[1,1,18,256,256]{4,3,2,1,0:T(8,128)S(1)} %bitcast.122), kind=kOutput, calls=%fused_computation.19 | convolution fusion | flops 3623878656 | bytes 9699328 | tf_op jit(solution)/shard_map/iwk,wkl->il/dot_general | solution.py:139
  86.0 9.5 %all-to-all-start.2 = ((f32[32,1,2]{2,1,0:T(1,128)}), f32[32,1,2]{2,1,0:T(1,128)S(1)}, u32[]{:S(2)}, u32[]{:S(2)}) async-start(f32[32,1,2]{2,1,0:T(1,128)} %broadcast_in_dim.14), calls=%async_computation.2 | async-start | bytes 32768 | tf_op jit(solution)/shard_map/all_to_all | solution.py:28
  95.5 3.0 %fusion.4 = f32[18,256]{1,0:T(8,128)S(1)} fusion(f32[1,1,18,256,256]{4,3,2,1,0:T(8,128)} %param.11, f32[256,256]{1,0:T(8,128)S(1)} %fusion.37), kind=kLoop, calls=%fused_computation.7 | loop fusion | flops 2354688 | bytes 4999168 | tf_op jit(solution)/shard_map/reduce_sum | solution.py:129
  98.5 6.7 %all-to-all-done.2 = f32[32,1,2]{2,1,0:T(1,128)S(1)} async-done(((f32[32,1,2]{2,1,0:T(1,128)}), f32[32,1,2]{2,1,0:T(1,128)S(1)}, u32[]{:S(2)}, u32[]{:S(2)}) %all-to-all-start.2) | async-done | bytes 288 | tf_op jit(solution)/shard_map/all_to_all | solution.py:28
  108.0 14.1 %all_to_all.38 = f32[32,8,256]{2,1,0:T(8,128)S(1)} all-to-all(f32[32,8,256]{2,1,0:T(8,128)S(1)} %fusion.17), channel_id=1, replica_groups=mesh['seg'=8,'sec'=32] {'sec'}, dimensions={0} | all-to-all | bytes 524288 | tf_op jit(solution)/shard_map/all_to_all | solution.py:35
  123.4 4.3 %all-to-all-start.4 = ((f32[32,8,256]{2,1,0:T(8,128)}), f32[32,8,256]{2,1,0:T(8,128)S(1)}, u32[]{:S(2)}, u32[]{:S(2)}) async-start(f32[32,8,256]{2,1,0:T(8,128)} %gather_fusion.1), calls=%async_computation.4 | async-start | bytes 524288 | tf_op jit(solution)/shard_map/all_to_all | solution.py:37
  127.8 6.0 %fusion.22 = f32[256,18,256]{2,0,1:T(8,128)S(1)} fusion(f32[256,18,256]{2,0,1:T(8,128)} %copy-done.1, f32[256,256]{1,0:T(8,128)S(1)} %get-tuple-element.20), kind=kOutput, calls=%fused_computation.37 | convolution fusion | flops 3623878656 | bytes 9699328 | tf_op jit(solution)/shard_map/iwj,jk->iwk/dot_general | solution.py:138
  133.8 4.1 %fusion.12 = f32[256,256]{1,0:T(8,128)S(1)} fusion(f32[256,18,256]{2,0,1:T(8,128)S(1)} %fusion.22, f32[1,1,18,256,256]{4,3,2,1,0:T(8,128)S(1)} %bitcast.124), kind=kOutput, calls=%fused_computation.20 | convolution fusion | flops 3623878656 | bytes 9699328 | tf_op jit(solution)/shard_map/iwk,wkl->il/dot_general | solution.py:139
  141.1 18.7 %all_to_all.39 = f32[32,1,2]{2,1,0:T(1,128)S(1)} all-to-all(f32[32,1,2]{2,1,0:T(1,128)S(1)} %broadcast_in_dim.15), channel_id=1, replica_groups=mesh['seg'=8,'sec'=32] {'sec'}, dimensions={0} | all-to-all | bytes 512 | tf_op jit(solution)/shard_map/all_to_all | solution.py:28
  163.1 12.8 %all_to_all.40 = f32[32,1,1]{2,1,0:T(1,128)S(1)} all-to-all(f32[32,1,1]{2,1,0:T(1,128)S(1)} %broadcast_in_dim.16), channel_id=1, replica_groups=mesh['seg'=8,'sec'=32] {'sec'}, dimensions={0} | all-to-all | bytes 256 | tf_op jit(solution)/shard_map/all_to_all | solution.py:28
  (54 shorter events, 21.7 us)
Async XLA Ops:
  0.0 83.1 %copy-start = (f32[1,1,256,256]{3,2,1,0:T(8,128)S(1)}, f32[1,1,256,256]{3,2,1,0:T(8,128)}, u32[]{:S(2)}) copy-start(f32[1,1,256,256]{3,2,1,0:T(8,128)} %param.14) | copy-start | bytes 786436
  1.7 18.1 %collective-permute-start = (f32[280,256]{1,0:T(8,128)S(1)}, f32[280,256]{1,0:T(8,128)S(1)}, u32[]{:S(2)}, u32[]{:S(2)}) collective-permute-start(f32[280,256]{1,0:T(8,128)S(1)} %select_maximum_fusion.2), channel_id=1, source_target_pairs={{0,32},{32,64},{64,96},{96,128},{128,160},{160,192},{192,224},{1,3... | collective-permute-start | bytes 860168 | tf_op jit(solution)/shard_map/ppermute | solution.py:18
  8.5 23.7 %all-to-all-start = ((f32[32,8,256]{2,1,0:T(8,128)}), f32[32,8,256]{2,1,0:T(8,128)S(1)}, u32[]{:S(2)}, u32[]{:S(2)}) async-start(f32[32,8,256]{2,1,0:T(8,128)} %fusion.19), calls=%async_computation | async-start | bytes 524288 | tf_op jit(solution)/shard_map/all_to_all | solution.py:35
  22.2 17.1 %collective-permute-start.1 = (f32[280,256]{1,0:T(8,128)S(1)}, f32[280,256]{1,0:T(8,128)S(1)}, u32[]{:S(2)}, u32[]{:S(2)}) collective-permute-start(f32[280,256]{1,0:T(8,128)S(1)} %select_maximum_fusion.1), channel_id=1, source_target_pairs={{0,64},{32,96},{64,128},{96,160},{128,192},{160,224},{1,65},{33,97... | collective-permute-start | bytes 860168 | tf_op jit(solution)/shard_map/ppermute | solution.py:18
  33.5 49.6 %all-to-all-start.1 = ((f32[32,8,256]{2,1,0:T(8,128)}), f32[32,8,256]{2,1,0:T(8,128)S(1)}, u32[]{:S(2)}, u32[]{:S(2)}) async-start(f32[32,8,256]{2,1,0:T(8,128)} %gather_fusion), calls=%async_computation.1 | async-start | bytes 524288 | tf_op jit(solution)/shard_map/all_to_all | solution.py:37
  39.9 12.0 %collective-permute-start.2 = (f32[280,256]{1,0:T(8,128)S(1)}, f32[280,256]{1,0:T(8,128)S(1)}, u32[]{:S(2)}, u32[]{:S(2)}) collective-permute-start(f32[280,256]{1,0:T(8,128)S(1)} %select_maximum_fusion), channel_id=1, source_target_pairs={{0,128},{32,160},{64,192},{96,224},{1,129},{33,161},{65,193},{97,2... | collective-permute-start | bytes 860168 | tf_op jit(solution)/shard_map/ppermute | solution.py:18
  67.4 6.9 %copy-start.2 = (f32[1,1,256,256]{3,2,1,0:T(8,128)S(1)}, f32[1,1,256,256]{3,2,1,0:T(8,128)}, u32[]{:S(2)}) copy-start(f32[1,1,256,256]{3,2,1,0:T(8,128)} %param.9) | copy-start | bytes 786436
  67.4 11.4 %slice-start = ((s8[4718592]{0:T(1024)(128)(4,1)}), s8[4194304]{0:T(1024)(128)(4,1)S(1)}, s32[]{:S(2)}) async-start(s8[4718592]{0:T(1024)(128)(4,1)} %bitcast.121), calls=%async_computation.7 | async-start | bytes 8388608
  72.1 2.1 %copy-start.1 = (f32[256,18,256]{2,0,1:T(8,128)}, f32[256,18,256]{2,0,1:T(8,128)S(1)}, u32[]{:S(2)}) copy-start(f32[256,18,256]{2,0,1:T(8,128)S(1)} %fusion.32) | copy-start | bytes 14155780
  74.2 4.5 %slice-start.1 = ((s8[4718592]{0:T(1024)(128)(4,1)}), s8[524288]{0:T(1024)(128)(4,1)S(1)}, s32[]{:S(2)}) async-start(s8[4718592]{0:T(1024)(128)(4,1)} %bitcast.121), calls=%async_computation.8 | async-start | bytes 1048576
  83.1 24.6 %copy-start.3 = (f32[1,1,256,256]{3,2,1,0:T(8,128)S(1)}, f32[1,1,256,256]{3,2,1,0:T(8,128)}, u32[]{:S(2)}) copy-start(f32[1,1,256,256]{3,2,1,0:T(8,128)} %param.15) | copy-start | bytes 786436
  86.0 19.3 %all-to-all-start.2 = ((f32[32,1,2]{2,1,0:T(1,128)}), f32[32,1,2]{2,1,0:T(1,128)S(1)}, u32[]{:S(2)}, u32[]{:S(2)}) async-start(f32[32,1,2]{2,1,0:T(1,128)} %broadcast_in_dim.14), calls=%async_computation.2 | async-start | bytes 32768 | tf_op jit(solution)/shard_map/all_to_all | solution.py:28
  122.1 11.6 %slice-start.2 = ((s8[4718592]{0:T(1024)(128)(4,1)}), s8[524288]{0:T(1024)(128)(4,1)S(1)}, s32[]{:S(2)}) async-start(s8[4718592]{0:T(1024)(128)(4,1)} %bitcast.123), calls=%async_computation.9 | async-start | bytes 1048576
  123.4 15.2 %all-to-all-start.4 = ((f32[32,8,256]{2,1,0:T(8,128)}), f32[32,8,256]{2,1,0:T(8,128)S(1)}, u32[]{:S(2)}, u32[]{:S(2)}) async-start(f32[32,8,256]{2,1,0:T(8,128)} %gather_fusion.1), calls=%async_computation.4 | async-start | bytes 524288 | tf_op jit(solution)/shard_map/all_to_all | solution.py:37
  127.7 6.0 %slice-start.3 = ((s8[4718592]{0:T(1024)(128)(4,1)}), s8[4194304]{0:T(1024)(128)(4,1)S(1)}, s32[]{:S(2)}) async-start(s8[4718592]{0:T(1024)(128)(4,1)} %bitcast.123), calls=%async_computation.10 | async-start | bytes 8388608
where the time goes:
time: 179 us; the launch traced here: 178 us
  blocking collectives  45.6 us (25%)
  matrix products  39.3 us (22%)
  starting transfers between devices  37.3 us (21%)
  waiting for transfers between devices  23.7 us (13%)
  other arithmetic  10.8 us (6%)
  local copies, waits for them, and re-layouts  9.31 us (5%)
  Pallas kernels  8.29 us (5%)
  between operations  3.63 us (2%)
    all_to_all x2, blocking collectives, sec_total(): return jnp.sum(lax.all_to_all(spread, 'sec', 0, 0, tiled=True), axis=0)  31.5 us
    all_to_all x1, blocking collectives, regroup(): held = lax.all_to_all(pieces, 'sec', 0, 0, tiled=True)  14.1 us
    all_to_all x1, starting transfers between devices, regroup(): held = lax.all_to_all(pieces, 'sec', 0, 0, tiled=True)  11.3 us
    dot_general x2, matrix products, apply_h(): inner = jnp.einsum('iwj,jk->iwk', left_env, vector, precision=HIGH)  10.5 us
    ppermute x3, waiting for transfers between devices, passed_along(): lax.ppermute(value, axis, [(source, source + steps) for source in range(i...  10.1 us
    all_to_all x2, starting transfers between devices, regroup(): back = lax.all_to_all(ordered, 'sec', 0, 0, tiled=True)  10.1 us
    all_to_all x1, starting transfers between devices, sec_total(): return jnp.sum(lax.all_to_all(spread, 'sec', 0, 0, tiled=True), axis=0)  9.51 us
    dot_general x12, matrix products, product(): return jnp.matmul(left, right, precision=HIGH)  9.12 us
  transfers between devices with their start and end apart: 7, of which 4 were waited for; matrix products, arithmetic and copies ran while one was open for 25% of the time, Pallas kernels for 5%

commit v1 on v0

--- a/solution.py
+++ b/solution.py
@@ -38,27 +38,44 @@
     return back.reshape(rows, cols)
 
 
-def _mix_kernel(mix_ref, source_ref, out_ref):
+def _mix_half_kernel(mix_ref, source_ref, blocks_ref, rows_ref, half_ref, diag_ref):
     channels = source_ref.shape[0]
+
+    @pl.when(pl.program_id(0) == 0)
+    def _():
+        diag_ref[...] = jnp.zeros_like(diag_ref)
+
+    blocks = blocks_ref[...]
+    tile_rows = rows_ref[...]
     for w in range(channels):
         acc = source_ref[0] * mix_ref[0, w]
         for u in range(1, channels):
             acc = acc + source_ref[u] * mix_ref[u, w]
-        out_ref[w] = acc
-
-
-def channel_mix(mix, source, rows=64):
+        part = jnp.dot(acc, blocks, precision=HIGH, preferred_element_type=jnp.float32)
+        half_ref[w] = part
+        diag_ref[w:w + 1, :] += jnp.sum(tile_rows * part, axis=0, keepdims=True)
+
+
+def mix_and_half(mix, source, blocks, rows=64):
     channels, height, width = source.shape
     return pl.pallas_call(
-        _mix_kernel,
+        _mix_half_kernel,
         grid=(height // rows,),
         in_specs=[
             pl.BlockSpec(memory_space=pltpu.SMEM),
             pl.BlockSpec((channels, rows, width), lambda i: (0, i, 0)),
+            pl.BlockSpec((height, width), lambda i: (0, 0)),
+            pl.BlockSpec((rows, width), lambda i: (i, 0)),
         ],
-        out_specs=pl.BlockSpec((channels, rows, width), lambda i: (0, i, 0)),
-        out_shape=jax.ShapeDtypeStruct(source.shape, source.dtype),
-    )(mix, source)
+        out_specs=[
+            pl.BlockSpec((channels, rows, width), lambda i: (0, i, 0)),
+            pl.BlockSpec((channels, width), lambda i: (0, 0)),
+        ],
+        out_shape=[
+            jax.ShapeDtypeStruct(source.shape, source.dtype),
+            jax.ShapeDtypeStruct((channels, width), source.dtype),
+        ],
+    )(mix, source, blocks, blocks)
 
 
 def prefix_scan(own_mix, own_blocks):
@@ -128,10 +145,8 @@
     eye_lanes = (places[:, None] == places[None, :]).astype(jnp.float32)
     right_diag = jnp.sum(right_side * eye_lanes, axis=2)
     prefix_mix, prefix_blocks = prefix_scan(own_mix, own_blocks)
-    mixed = channel_mix(prefix_mix, boundary)
-    half = jnp.einsum("wkl,lj->wkj", mixed, prefix_blocks, precision=HIGH)
+    half, left_diag = mix_and_half(prefix_mix, boundary, prefix_blocks)
     left_env = jnp.einsum("ki,wkj->iwj", prefix_blocks, half, precision=HIGH)
-    left_diag = jnp.sum(prefix_blocks[None] * half, axis=1)
     diagonal = jnp.einsum("wi,wj->ij", left_diag, right_diag, precision=HIGH)
 
     def apply_h(vector, moved):

time: 179 us -> 184 us (1.028)
  Pallas kernels: 8.29 us -> 16.6 us
  matrix products: 39.3 us -> 35.4 us
    pallas_call x1, Pallas kernels: 8.29 us -> 16.6 us  [mix_and_half(): pl.pallas_call(_mix_half_kernel, grid=(height // rows,), in_specs=[pl.Blo...]
    dot_general x1 -> x0, matrix products: 6.08 us -> none  [per_device(): half = jnp.einsum('wkl,lj->wkj', mixed, prefix_blocks, precision=HIGH)]
  transfers between devices with their start and end apart: 7 -> 7, of which waited for: 4 -> 4; matrix products, arithmetic and copies ran while one was open for 25% -> 22% of each run, Pallas kernels for 5% -> 9%
where the time goes in v1:
time: 184 us; the launch traced here: 183 us
  blocking collectives  45.6 us (25%)
  starting transfers between devices  37.5 us (20%)
  matrix products  35.4 us (19%)
  waiting for transfers between devices  23.5 us (13%)
  Pallas kernels  16.6 us (9%)
  other arithmetic  10.8 us (6%)
  local copies, waits for them, and re-layouts  9.49 us (5%)
  between operations  3.84 us (2%)
    all_to_all x2, blocking collectives, sec_total(): return jnp.sum(lax.all_to_all(spread, 'sec', 0, 0, tiled=True), axis=0)  31.5 us
    pallas_call x1, Pallas kernels, mix_and_half(): pl.pallas_call(_mix_half_kernel, grid=(height // rows,), in_specs=[pl.Blo...  16.6 us
    all_to_all x1, blocking collectives, regroup(): held = lax.all_to_all(pieces, 'sec', 0, 0, tiled=True)  14.1 us
    all_to_all x1, starting transfers between devices, regroup(): held = lax.all_to_all(pieces, 'sec', 0, 0, tiled=True)  11.3 us
    dot_general x2, matrix products, apply_h(): inner = jnp.einsum('iwj,jk->iwk', left_env, vector, precision=HIGH)  10.5 us
    all_to_all x2, starting transfers between devices, regroup(): back = lax.all_to_all(ordered, 'sec', 0, 0, tiled=True)  10.3 us
    ppermute x3, waiting for transfers between devices, passed_along(): lax.ppermute(value, axis, [(source, source + steps) for source in range(i...  10.1 us
    dot_general x12, matrix products, product(): return jnp.matmul(left, right, precision=HIGH)  9.84 us
  transfers between devices with their start and end apart: 7, of which 4 were waited for; matrix products, arithmetic and copies ran while one was open for 22% of the time, Pallas kernels for 9%

profile of v1, /device:TPU:16, one launch (start us, length us, event | category | flops | bytes accessed | tf_op | source)
XLA Modules:
  0.0 182.7 jit_solution(12306226903930625450)
XLA Ops:
  1.7 1.9 %collective-permute-start = (f32[280,256]{1,0:T(8,128)S(1)}, f32[280,256]{1,0:T(8,128)S(1)}, u32[]{:S(2)}, u32[]{:S(2)}) collective-permute-start(f32[280,256]{1,0:T(8,128)S(1)} %select_maximum_fusion.2), channel_id=1, source_target_pairs={{0,32},{32,64},{64,96},{96,128},{128,160},{160,192},{192,224},{1,3... | collective-permute-start | bytes 860168 | tf_op jit(solution)/shard_map/ppermute | solution.py:18
  3.7 1.3 constant_dynamic-slice_fusion.1
  6.2 2.2 %fusion.19 = f32[32,8,256]{2,1,0:T(8,128)} fusion(f32[1,1,256,256]{3,2,1,0:T(8,128)} %param.15, f32[1,1,256,256]{3,2,1,0:T(8,128)} %param.9, f32[256]{0:T(256)S(1)} %get-tuple-element.25, f32[256]{0:T(256)S(1)} %get-tuple-element.26), kind=kOutput, calls=%fused_computation.33 | convolution fusion | flops 201457664 | bytes 788480 | tf_op jit(solution)/shard_map/dot_general | solution.py:22
  8.4 11.3 %all-to-all-start = ((f32[32,8,256]{2,1,0:T(8,128)}), f32[32,8,256]{2,1,0:T(8,128)S(1)}, u32[]{:S(2)}, u32[]{:S(2)}) async-start(f32[32,8,256]{2,1,0:T(8,128)} %fusion.19), calls=%async_computation | async-start | bytes 524288 | tf_op jit(solution)/shard_map/all_to_all | solution.py:35
  19.7 1.4 convolution_select_fusion.3
  22.1 3.2 %collective-permute-start.1 = (f32[280,256]{1,0:T(8,128)S(1)}, f32[280,256]{1,0:T(8,128)S(1)}, u32[]{:S(2)}, u32[]{:S(2)}) collective-permute-start(f32[280,256]{1,0:T(8,128)S(1)} %select_maximum_fusion.1), channel_id=1, source_target_pairs={{0,64},{32,96},{64,128},{96,160},{128,192},{160,224},{1,65},{33,97... | collective-permute-start | bytes 860168 | tf_op jit(solution)/shard_map/ppermute | solution.py:18
  26.0 6.1 %all-to-all-done = f32[32,8,256]{2,1,0:T(8,128)S(1)} async-done(((f32[32,8,256]{2,1,0:T(8,128)}), f32[32,8,256]{2,1,0:T(8,128)S(1)}, u32[]{:S(2)}, u32[]{:S(2)}) %all-to-all-start) | async-done | bytes 262176 | tf_op jit(solution)/shard_map/all_to_all | solution.py:35
  33.4 5.8 %all-to-all-start.1 = ((f32[32,8,256]{2,1,0:T(8,128)}), f32[32,8,256]{2,1,0:T(8,128)S(1)}, u32[]{:S(2)}, u32[]{:S(2)}) async-start(f32[32,8,256]{2,1,0:T(8,128)} %gather_fusion), calls=%async_computation.1 | async-start | bytes 524288 | tf_op jit(solution)/shard_map/all_to_all | solution.py:37
  41.6 10.1 %collective-permute-done.2 = f32[280,256]{1,0:T(8,128)S(1)} collective-permute-done((f32[280,256]{1,0:T(8,128)S(1)}, f32[280,256]{1,0:T(8,128)S(1)}, u32[]{:S(2)}, u32[]{:S(2)}) %collective-permute-start.2) | collective-permute-done | bytes 286752 | tf_op jit(solution)/shard_map/ppermute | solution.py:18
  53.6 16.6 %shard_map.91 = (f32[18,256,256]{2,1,0:T(8,128)}, f32[18,256]{1,0:T(8,128)}) custom-call(f32[18,18]{1,0:T(8,128)} %convolution_select_fusion.4.mix_ref, f32[18,256,256]{2,1,0:T(8,128)} %bitcast.119, f32[256,256]{1,0:T(8,128)} %convolution_select_fusion.blocks_ref.rows_ref, f32[256,256]{1,0:T(8,128)} %convolution_select_fusion.blocks_ref.rows_ref), custom_call_target="tpu_custom_call" | custom-call | tf_op jit(solution)/shard_map/pallas_call | solution.py:61
  70.2 6.4 %fusion.30 = f32[256,18,256]{2,0,1:T(8,128)S(1)} fusion(f32[18,256,256]{2,1,0:T(8,128)} %get-tuple-element.7, f32[256,256]{1,0:T(8,128)S(1)} %copy-done.2), kind=kOutput, calls=%fused_computation.44 | convolution fusion | flops 3623878656 | bytes 9699328 | tf_op jit(solution)/shard_map/ki,wkj->iwj/dot_general | solution.py:149
  76.6 2.1 %copy-done.1 = f32[256,18,256]{2,0,1:T(8,128)} copy-done((f32[256,18,256]{2,0,1:T(8,128)}, f32[256,18,256]{2,0,1:T(8,128)S(1)}, u32[]{:S(2)}) %copy-start.1) | copy-done | bytes 4718616
  78.8 4.5 %fusion.28 = f32[256,18,256]{2,0,1:T(8,128)S(1)} fusion(f32[256,18,256]{2,0,1:T(8,128)S(1)} %fusion.30, f32[1,1,256,256]{3,2,1,0:T(8,128)S(1)} %copy-done.3, f32[256]{0:T(256)S(1)} %get-tuple-element.25, f32[256]{0:T(256)S(1)} %get-tuple-element.26), kind=kOutput, calls=%fused_computation.42 | convolution fusion | flops 3624009728 | bytes 9701376 | tf_op jit(solution)/shard_map/iwj,jk->iwk/dot_general | solution.py:153
  83.3 4.0 %fusion.9 = f32[256,256]{1,0:T(8,128)S(1)} fusion(f32[256,18,256]{2,0,1:T(8,128)S(1)} %fusion.28, f32[1,1,18,256,256]{4,3,2,1,0:T(8,128)S(1)} %bitcast.116), kind=kOutput, calls=%fused_computation.18 | convolution fusion | flops 3623878656 | bytes 9699328 | tf_op jit(solution)/shard_map/iwk,wkl->il/dot_general | solution.py:154
  88.4 1.4 pad_maximum_fusion
  90.5 9.5 %all-to-all-start.2 = ((f32[32,1,2]{2,1,0:T(1,128)}), f32[32,1,2]{2,1,0:T(1,128)S(1)}, u32[]{:S(2)}, u32[]{:S(2)}) async-start(f32[32,1,2]{2,1,0:T(1,128)} %broadcast_in_dim.14), calls=%async_computation.2 | async-start | bytes 32768 | tf_op jit(solution)/shard_map/all_to_all | solution.py:28
  100.0 3.0 %fusion.4 = f32[18,256]{1,0:T(8,128)S(1)} fusion(f32[1,1,18,256,256]{4,3,2,1,0:T(8,128)} %param.11, f32[256,256]{1,0:T(8,128)S(1)} %fusion.35), kind=kLoop, calls=%fused_computation.7 | loop fusion | flops 2354688 | bytes 4999168 | tf_op jit(solution)/shard_map/reduce_sum | solution.py:146
  103.0 6.7 %all-to-all-done.2 = f32[32,1,2]{2,1,0:T(1,128)S(1)} async-done(((f32[32,1,2]{2,1,0:T(1,128)}), f32[32,1,2]{2,1,0:T(1,128)S(1)}, u32[]{:S(2)}, u32[]{:S(2)}) %all-to-all-start.2) | async-done | bytes 288 | tf_op jit(solution)/shard_map/all_to_all | solution.py:28
  112.7 14.1 %all_to_all.38 = f32[32,8,256]{2,1,0:T(8,128)S(1)} all-to-all(f32[32,8,256]{2,1,0:T(8,128)S(1)} %fusion.17), channel_id=1, replica_groups=mesh['seg'=8,'sec'=32] {'sec'}, dimensions={0} | all-to-all | bytes 524288 | tf_op jit(solution)/shard_map/all_to_all | solution.py:35
  128.1 4.5 %all-to-all-start.4 = ((f32[32,8,256]{2,1,0:T(8,128)}), f32[32,8,256]{2,1,0:T(8,128)S(1)}, u32[]{:S(2)}, u32[]{:S(2)}) async-start(f32[32,8,256]{2,1,0:T(8,128)} %gather_fusion.1), calls=%async_computation.4 | async-start | bytes 524288 | tf_op jit(solution)/shard_map/all_to_all | solution.py:37
  132.7 6.0 %fusion.22 = f32[256,18,256]{2,0,1:T(8,128)S(1)} fusion(f32[256,18,256]{2,0,1:T(8,128)} %copy-done.1, f32[256,256]{1,0:T(8,128)S(1)} %get-tuple-element.22), kind=kOutput, calls=%fused_computation.36 | convolution fusion | flops 3623878656 | bytes 9699328 | tf_op jit(solution)/shard_map/iwj,jk->iwk/dot_general | solution.py:153
  138.7 4.1 %fusion.12 = f32[256,256]{1,0:T(8,128)S(1)} fusion(f32[256,18,256]{2,0,1:T(8,128)S(1)} %fusion.22, f32[1,1,18,256,256]{4,3,2,1,0:T(8,128)S(1)} %bitcast.118), kind=kOutput, calls=%fused_computation.19 | convolution fusion | flops 3623878656 | bytes 9699328 | tf_op jit(solution)/shard_map/iwk,wkl->il/dot_general | solution.py:154
  145.6 18.7 %all_to_all.39 = f32[32,1,2]{2,1,0:T(1,128)S(1)} all-to-all(f32[32,1,2]{2,1,0:T(1,128)S(1)} %broadcast_in_dim.15), channel_id=1, replica_groups=mesh['seg'=8,'sec'=32] {'sec'}, dimensions={0} | all-to-all | bytes 512 | tf_op jit(solution)/shard_map/all_to_all | solution.py:28
  167.9 12.8 %all_to_all.40 = f32[32,1,1]{2,1,0:T(1,128)S(1)} all-to-all(f32[32,1,1]{2,1,0:T(1,128)S(1)} %broadcast_in_dim.16), channel_id=1, replica_groups=mesh['seg'=8,'sec'=32] {'sec'}, dimensions={0} | all-to-all | bytes 256 | tf_op jit(solution)/shard_map/all_to_all | solution.py:28
  (57 shorter events, 21.0 us)
Async XLA Ops:
  0.0 87.4 %copy-start = (f32[1,1,256,256]{3,2,1,0:T(8,128)S(1)}, f32[1,1,256,256]{3,2,1,0:T(8,128)}, u32[]{:S(2)}) copy-start(f32[1,1,256,256]{3,2,1,0:T(8,128)} %param.14) | copy-start | bytes 786436
  1.7 18.0 %collective-permute-start = (f32[280,256]{1,0:T(8,128)S(1)}, f32[280,256]{1,0:T(8,128)S(1)}, u32[]{:S(2)}, u32[]{:S(2)}) collective-permute-start(f32[280,256]{1,0:T(8,128)S(1)} %select_maximum_fusion.2), channel_id=1, source_target_pairs={{0,32},{32,64},{64,96},{96,128},{128,160},{160,192},{192,224},{1,3... | collective-permute-start | bytes 860168 | tf_op jit(solution)/shard_map/ppermute | solution.py:18
  8.4 23.7 %all-to-all-start = ((f32[32,8,256]{2,1,0:T(8,128)}), f32[32,8,256]{2,1,0:T(8,128)S(1)}, u32[]{:S(2)}, u32[]{:S(2)}) async-start(f32[32,8,256]{2,1,0:T(8,128)} %fusion.19), calls=%async_computation | async-start | bytes 524288 | tf_op jit(solution)/shard_map/all_to_all | solution.py:35
  22.1 17.1 %collective-permute-start.1 = (f32[280,256]{1,0:T(8,128)S(1)}, f32[280,256]{1,0:T(8,128)S(1)}, u32[]{:S(2)}, u32[]{:S(2)}) collective-permute-start(f32[280,256]{1,0:T(8,128)S(1)} %select_maximum_fusion.1), channel_id=1, source_target_pairs={{0,64},{32,96},{64,128},{96,160},{128,192},{160,224},{1,65},{33,97... | collective-permute-start | bytes 860168 | tf_op jit(solution)/shard_map/ppermute | solution.py:18
  33.4 54.0 %all-to-all-start.1 = ((f32[32,8,256]{2,1,0:T(8,128)}), f32[32,8,256]{2,1,0:T(8,128)S(1)}, u32[]{:S(2)}, u32[]{:S(2)}) async-start(f32[32,8,256]{2,1,0:T(8,128)} %gather_fusion), calls=%async_computation.1 | async-start | bytes 524288 | tf_op jit(solution)/shard_map/all_to_all | solution.py:37
  39.7 12.0 %collective-permute-start.2 = (f32[280,256]{1,0:T(8,128)S(1)}, f32[280,256]{1,0:T(8,128)S(1)}, u32[]{:S(2)}, u32[]{:S(2)}) collective-permute-start(f32[280,256]{1,0:T(8,128)S(1)} %select_maximum_fusion), channel_id=1, source_target_pairs={{0,128},{32,160},{64,192},{96,224},{1,129},{33,161},{65,193},{97,2... | collective-permute-start | bytes 860168 | tf_op jit(solution)/shard_map/ppermute | solution.py:18
  53.6 16.6 %copy-start.2 = (f32[256,256]{1,0:T(8,128)S(1)}, f32[256,256]{1,0:T(8,128)}, u32[]{:S(2)}) copy-start(f32[256,256]{1,0:T(8,128)} %convolution_select_fusion.blocks_ref.rows_ref) | copy-start | bytes 786436
  70.1 8.6 %copy-start.3 = (f32[1,1,256,256]{3,2,1,0:T(8,128)S(1)}, f32[1,1,256,256]{3,2,1,0:T(8,128)}, u32[]{:S(2)}) copy-start(f32[1,1,256,256]{3,2,1,0:T(8,128)} %param.9) | copy-start | bytes 786436
  70.1 13.1 %slice-start = ((s8[4718592]{0:T(1024)(128)(4,1)}), s8[4194304]{0:T(1024)(128)(4,1)S(1)}, s32[]{:S(2)}) async-start(s8[4718592]{0:T(1024)(128)(4,1)} %bitcast.115), calls=%async_computation.7 | async-start | bytes 8388608
  76.6 2.1 %copy-start.1 = (f32[256,18,256]{2,0,1:T(8,128)}, f32[256,18,256]{2,0,1:T(8,128)S(1)}, u32[]{:S(2)}) copy-start(f32[256,18,256]{2,0,1:T(8,128)S(1)} %fusion.30) | copy-start | bytes 14155780
  78.7 4.5 %slice-start.1 = ((s8[4718592]{0:T(1024)(128)(4,1)}), s8[524288]{0:T(1024)(128)(4,1)S(1)}, s32[]{:S(2)}) async-start(s8[4718592]{0:T(1024)(128)(4,1)} %bitcast.115), calls=%async_computation.8 | async-start | bytes 1048576
  87.3 24.5 %copy-start.5 = (f32[18,256]{1,0:T(8,128)S(1)}, f32[18,256]{1,0:T(8,128)}, u32[]{:S(2)}) copy-start(f32[18,256]{1,0:T(8,128)} %get-tuple-element.8) | copy-start | bytes 55300
  87.3 25.0 %copy-start.4 = (f32[1,1,256,256]{3,2,1,0:T(8,128)S(1)}, f32[1,1,256,256]{3,2,1,0:T(8,128)}, u32[]{:S(2)}) copy-start(f32[1,1,256,256]{3,2,1,0:T(8,128)} %param.15) | copy-start | bytes 786436
  90.5 19.3 %all-to-all-start.2 = ((f32[32,1,2]{2,1,0:T(1,128)}), f32[32,1,2]{2,1,0:T(1,128)S(1)}, u32[]{:S(2)}, u32[]{:S(2)}) async-start(f32[32,1,2]{2,1,0:T(1,128)} %broadcast_in_dim.14), calls=%async_computation.2 | async-start | bytes 32768 | tf_op jit(solution)/shard_map/all_to_all | solution.py:28
  126.9 11.9 %slice-start.2 = ((s8[4718592]{0:T(1024)(128)(4,1)}), s8[524288]{0:T(1024)(128)(4,1)S(1)}, s32[]{:S(2)}) async-start(s8[4718592]{0:T(1024)(128)(4,1)} %bitcast.117), calls=%async_computation.9 | async-start | bytes 1048576
  128.1 15.2 %all-to-all-start.4 = ((f32[32,8,256]{2,1,0:T(8,128)}), f32[32,8,256]{2,1,0:T(8,128)S(1)}, u32[]{:S(2)}, u32[]{:S(2)}) async-start(f32[32,8,256]{2,1,0:T(8,128)} %gather_fusion.1), calls=%async_computation.4 | async-start | bytes 524288 | tf_op jit(solution)/shard_map/all_to_all | solution.py:37
  132.7 6.0 %slice-start.3 = ((s8[4718592]{0:T(1024)(128)(4,1)}), s8[4194304]{0:T(1024)(128)(4,1)S(1)}, s32[]{:S(2)}) async-start(s8[4718592]{0:T(1024)(128)(4,1)} %bitcast.117), calls=%async_computation.10 | async-start | bytes 8388608

commit v2 on v0

--- a/solution.py
+++ b/solution.py
@@ -39,12 +39,19 @@
 
 
 def _mix_kernel(mix_ref, source_ref, out_ref):
-    channels = source_ref.shape[0]
-    for w in range(channels):
-        acc = source_ref[0] * mix_ref[0, w]
-        for u in range(1, channels):
-            acc = acc + source_ref[u] * mix_ref[u, w]
-        out_ref[w] = acc
+    channels, rows, width = source_ref.shape
+
+    def body(t, carry):
+        r = pl.multiple_of(t * 8, 8)
+        parts = [source_ref[u, pl.ds(r, 8), :] for u in range(channels)]
+        for w in range(channels):
+            acc = parts[0] * mix_ref[0, w]
+            for u in range(1, channels):
+                acc = acc + parts[u] * mix_ref[u, w]
+            out_ref[w, pl.ds(r, 8), :] = acc
+        return carry
+
+    lax.fori_loop(0, rows // 8, body, 0)
 
 
 def channel_mix(mix, source, rows=64):

time: 179 us -> 181 us (1.011)
  transfers between devices with their start and end apart: 7 -> 7, of which waited for: 4 -> 4; matrix products, arithmetic and copies ran while one was open for 25% -> 25% of each run, Pallas kernels for 5% -> 6%
where the time goes in v2:
time: 181 us; the launch traced here: 180 us
  blocking collectives  45.6 us (25%)
  matrix products  39.3 us (22%)
  starting transfers between devices  37.3 us (21%)
  waiting for transfers between devices  23.7 us (13%)
  other arithmetic  10.8 us (6%)
  Pallas kernels  10 us (6%)
  local copies, waits for them, and re-layouts  9.31 us (5%)
  between operations  3.63 us (2%)
    all_to_all x2, blocking collectives, sec_total(): return jnp.sum(lax.all_to_all(spread, 'sec', 0, 0, tiled=True), axis=0)  31.5 us
    all_to_all x1, blocking collectives, regroup(): held = lax.all_to_all(pieces, 'sec', 0, 0, tiled=True)  14.1 us
    all_to_all x1, starting transfers between devices, regroup(): held = lax.all_to_all(pieces, 'sec', 0, 0, tiled=True)  11.3 us
    dot_general x2, matrix products, apply_h(): inner = jnp.einsum('iwj,jk->iwk', left_env, vector, precision=HIGH)  10.5 us
    ppermute x3, waiting for transfers between devices, passed_along(): lax.ppermute(value, axis, [(source, source + steps) for source in range(i...  10.1 us
    all_to_all x2, starting transfers between devices, regroup(): back = lax.all_to_all(ordered, 'sec', 0, 0, tiled=True)  10.1 us
    pallas_call x1, Pallas kernels, channel_mix(): pl.pallas_call(_mix_kernel, grid=(height // rows,), in_specs=[pl.BlockSpe...  10 us
    all_to_all x1, starting transfers between devices, sec_total(): return jnp.sum(lax.all_to_all(spread, 'sec', 0, 0, tiled=True), axis=0)  9.51 us
  transfers between devices with their start and end apart: 7, of which 4 were waited for; matrix products, arithmetic and copies ran while one was open for 25% of the time, Pallas kernels for 6%

profile of v2, /device:TPU:16, one launch (start us, length us, event | category | flops | bytes accessed | tf_op | source)
XLA Modules:
  0.0 179.7 jit_solution(16303985120232870169)
XLA Ops:
  1.7 1.9 %collective-permute-start = (f32[280,256]{1,0:T(8,128)S(1)}, f32[280,256]{1,0:T(8,128)S(1)}, u32[]{:S(2)}, u32[]{:S(2)}) collective-permute-start(f32[280,256]{1,0:T(8,128)S(1)} %select_maximum_fusion.2), channel_id=1, source_target_pairs={{0,32},{32,64},{64,96},{96,128},{128,160},{160,192},{192,224},{1,3... | collective-permute-start | bytes 860168 | tf_op jit(solution)/shard_map/ppermute | solution.py:18
  3.7 1.4 constant_dynamic-slice_fusion.1
  6.3 2.2 %fusion.19 = f32[32,8,256]{2,1,0:T(8,128)} fusion(f32[1,1,256,256]{3,2,1,0:T(8,128)} %param.15, f32[1,1,256,256]{3,2,1,0:T(8,128)} %param.9, f32[256]{0:T(256)S(1)} %get-tuple-element.23, f32[256]{0:T(256)S(1)} %get-tuple-element.24), kind=kOutput, calls=%fused_computation.34 | convolution fusion | flops 201457664 | bytes 788480 | tf_op jit(solution)/shard_map/dot_general | solution.py:22
  8.5 11.3 %all-to-all-start = ((f32[32,8,256]{2,1,0:T(8,128)}), f32[32,8,256]{2,1,0:T(8,128)S(1)}, u32[]{:S(2)}, u32[]{:S(2)}) async-start(f32[32,8,256]{2,1,0:T(8,128)} %fusion.19), calls=%async_computation | async-start | bytes 524288 | tf_op jit(solution)/shard_map/all_to_all | solution.py:35
  19.8 1.4 convolution_select_fusion.3
  22.2 3.2 %collective-permute-start.1 = (f32[280,256]{1,0:T(8,128)S(1)}, f32[280,256]{1,0:T(8,128)S(1)}, u32[]{:S(2)}, u32[]{:S(2)}) collective-permute-start(f32[280,256]{1,0:T(8,128)S(1)} %select_maximum_fusion.1), channel_id=1, source_target_pairs={{0,64},{32,96},{64,128},{96,160},{128,192},{160,224},{1,65},{33,97... | collective-permute-start | bytes 860168 | tf_op jit(solution)/shard_map/ppermute | solution.py:18
  26.1 6.1 %all-to-all-done = f32[32,8,256]{2,1,0:T(8,128)S(1)} async-done(((f32[32,8,256]{2,1,0:T(8,128)}), f32[32,8,256]{2,1,0:T(8,128)S(1)}, u32[]{:S(2)}, u32[]{:S(2)}) %all-to-all-start) | async-done | bytes 262176 | tf_op jit(solution)/shard_map/all_to_all | solution.py:35
  33.5 5.8 %all-to-all-start.1 = ((f32[32,8,256]{2,1,0:T(8,128)}), f32[32,8,256]{2,1,0:T(8,128)S(1)}, u32[]{:S(2)}, u32[]{:S(2)}) async-start(f32[32,8,256]{2,1,0:T(8,128)} %gather_fusion), calls=%async_computation.1 | async-start | bytes 524288 | tf_op jit(solution)/shard_map/all_to_all | solution.py:37
  41.7 10.1 %collective-permute-done.2 = f32[280,256]{1,0:T(8,128)S(1)} collective-permute-done((f32[280,256]{1,0:T(8,128)S(1)}, f32[280,256]{1,0:T(8,128)S(1)}, u32[]{:S(2)}, u32[]{:S(2)}) %collective-permute-start.2) | collective-permute-done | bytes 286752 | tf_op jit(solution)/shard_map/ppermute | solution.py:18
  52.6 10.0 %shard_map.91 = f32[18,256,256]{2,1,0:T(8,128)} custom-call(f32[18,18]{1,0:T(8,128)} %convolution_select_fusion.4.mix_ref, f32[18,256,256]{2,1,0:T(8,128)} %bitcast.125), custom_call_target="tpu_custom_call" | custom-call | tf_op jit(solution)/shard_map/pallas_call | solution.py:59
  63.0 6.1 %multiply_reduce_fusion = (f32[18,256]{1,0:T(8,128)S(1)}, f32[18,256,256]{2,1,0:T(8,128)S(1)}) fusion(f32[256,256]{1,0:T(8,128)S(1)} %convolution_select_fusion, f32[18,256,256]{2,1,0:T(8,128)} %shard_map.91), kind=kOutput, calls=%fused_computation.8 | convolution fusion | flops 3626233344 | bytes 9717760 | tf_op jit(solution)/shard_map/wkl,lj->wkj/dot_general | solution.py:139
  69.1 4.7 %fusion.32 = f32[256,18,256]{2,0,1:T(8,128)S(1)} fusion(f32[18,256,256]{2,1,0:T(8,128)S(1)} %get-tuple-element.19, f32[256,256]{1,0:T(8,128)S(1)} %convolution_select_fusion), kind=kOutput, calls=%fused_computation.47 | convolution fusion | flops 3623878656 | bytes 9699328 | tf_op jit(solution)/shard_map/ki,wkj->iwj/dot_general | solution.py:140
  73.9 2.1 %copy-done.1 = f32[256,18,256]{2,0,1:T(8,128)} copy-done((f32[256,18,256]{2,0,1:T(8,128)}, f32[256,18,256]{2,0,1:T(8,128)S(1)}, u32[]{:S(2)}) %copy-start.1) | copy-done | bytes 4718616
  76.0 4.5 %fusion.28 = f32[256,18,256]{2,0,1:T(8,128)S(1)} fusion(f32[256,18,256]{2,0,1:T(8,128)S(1)} %fusion.32, f32[1,1,256,256]{3,2,1,0:T(8,128)S(1)} %copy-done.2, f32[256]{0:T(256)S(1)} %get-tuple-element.23, f32[256]{0:T(256)S(1)} %get-tuple-element.24), kind=kOutput, calls=%fused_computation.43 | convolution fusion | flops 3624009728 | bytes 9701376 | tf_op jit(solution)/shard_map/iwj,jk->iwk/dot_general | solution.py:145
  80.5 4.3 %fusion.9 = f32[256,256]{1,0:T(8,128)S(1)} fusion(f32[256,18,256]{2,0,1:T(8,128)S(1)} %fusion.28, f32[1,1,18,256,256]{4,3,2,1,0:T(8,128)S(1)} %bitcast.122), kind=kOutput, calls=%fused_computation.19 | convolution fusion | flops 3623878656 | bytes 9699328 | tf_op jit(solution)/shard_map/iwk,wkl->il/dot_general | solution.py:146
  87.7 9.5 %all-to-all-start.2 = ((f32[32,1,2]{2,1,0:T(1,128)}), f32[32,1,2]{2,1,0:T(1,128)S(1)}, u32[]{:S(2)}, u32[]{:S(2)}) async-start(f32[32,1,2]{2,1,0:T(1,128)} %broadcast_in_dim.14), calls=%async_computation.2 | async-start | bytes 32768 | tf_op jit(solution)/shard_map/all_to_all | solution.py:28
  97.2 3.0 %fusion.4 = f32[18,256]{1,0:T(8,128)S(1)} fusion(f32[1,1,18,256,256]{4,3,2,1,0:T(8,128)} %param.11, f32[256,256]{1,0:T(8,128)S(1)} %fusion.37), kind=kLoop, calls=%fused_computation.7 | loop fusion | flops 2354688 | bytes 4999168 | tf_op jit(solution)/shard_map/reduce_sum | solution.py:136
  100.3 6.7 %all-to-all-done.2 = f32[32,1,2]{2,1,0:T(1,128)S(1)} async-done(((f32[32,1,2]{2,1,0:T(1,128)}), f32[32,1,2]{2,1,0:T(1,128)S(1)}, u32[]{:S(2)}, u32[]{:S(2)}) %all-to-all-start.2) | async-done | bytes 288 | tf_op jit(solution)/shard_map/all_to_all | solution.py:28
  109.7 14.1 %all_to_all.38 = f32[32,8,256]{2,1,0:T(8,128)S(1)} all-to-all(f32[32,8,256]{2,1,0:T(8,128)S(1)} %fusion.17), channel_id=1, replica_groups=mesh['seg'=8,'sec'=32] {'sec'}, dimensions={0} | all-to-all | bytes 524288 | tf_op jit(solution)/shard_map/all_to_all | solution.py:35
  125.2 4.3 %all-to-all-start.4 = ((f32[32,8,256]{2,1,0:T(8,128)}), f32[32,8,256]{2,1,0:T(8,128)S(1)}, u32[]{:S(2)}, u32[]{:S(2)}) async-start(f32[32,8,256]{2,1,0:T(8,128)} %gather_fusion.1), calls=%async_computation.4 | async-start | bytes 524288 | tf_op jit(solution)/shard_map/all_to_all | solution.py:37
  129.5 6.0 %fusion.22 = f32[256,18,256]{2,0,1:T(8,128)S(1)} fusion(f32[256,18,256]{2,0,1:T(8,128)} %copy-done.1, f32[256,256]{1,0:T(8,128)S(1)} %get-tuple-element.20), kind=kOutput, calls=%fused_computation.37 | convolution fusion | flops 3623878656 | bytes 9699328 | tf_op jit(solution)/shard_map/iwj,jk->iwk/dot_general | solution.py:145
  135.5 4.1 %fusion.12 = f32[256,256]{1,0:T(8,128)S(1)} fusion(f32[256,18,256]{2,0,1:T(8,128)S(1)} %fusion.22, f32[1,1,18,256,256]{4,3,2,1,0:T(8,128)S(1)} %bitcast.124), kind=kOutput, calls=%fused_computation.20 | convolution fusion | flops 3623878656 | bytes 9699328 | tf_op jit(solution)/shard_map/iwk,wkl->il/dot_general | solution.py:146
  142.8 18.7 %all_to_all.39 = f32[32,1,2]{2,1,0:T(1,128)S(1)} all-to-all(f32[32,1,2]{2,1,0:T(1,128)S(1)} %broadcast_in_dim.15), channel_id=1, replica_groups=mesh['seg'=8,'sec'=32] {'sec'}, dimensions={0} | all-to-all | bytes 512 | tf_op jit(solution)/shard_map/all_to_all | solution.py:28
  164.8 12.8 %all_to_all.40 = f32[32,1,1]{2,1,0:T(1,128)S(1)} all-to-all(f32[32,1,1]{2,1,0:T(1,128)S(1)} %broadcast_in_dim.16), channel_id=1, replica_groups=mesh['seg'=8,'sec'=32] {'sec'}, dimensions={0} | all-to-all | bytes 256 | tf_op jit(solution)/shard_map/all_to_all | solution.py:28
  (54 shorter events, 21.7 us)
Async XLA Ops:
  0.0 84.8 %copy-start = (f32[1,1,256,256]{3,2,1,0:T(8,128)S(1)}, f32[1,1,256,256]{3,2,1,0:T(8,128)}, u32[]{:S(2)}) copy-start(f32[1,1,256,256]{3,2,1,0:T(8,128)} %param.14) | copy-start | bytes 786436
  1.7 18.1 %collective-permute-start = (f32[280,256]{1,0:T(8,128)S(1)}, f32[280,256]{1,0:T(8,128)S(1)}, u32[]{:S(2)}, u32[]{:S(2)}) collective-permute-start(f32[280,256]{1,0:T(8,128)S(1)} %select_maximum_fusion.2), channel_id=1, source_target_pairs={{0,32},{32,64},{64,96},{96,128},{128,160},{160,192},{192,224},{1,3... | collective-permute-start | bytes 860168 | tf_op jit(solution)/shard_map/ppermute | solution.py:18
  8.5 23.7 %all-to-all-start = ((f32[32,8,256]{2,1,0:T(8,128)}), f32[32,8,256]{2,1,0:T(8,128)S(1)}, u32[]{:S(2)}, u32[]{:S(2)}) async-start(f32[32,8,256]{2,1,0:T(8,128)} %fusion.19), calls=%async_computation | async-start | bytes 524288 | tf_op jit(solution)/shard_map/all_to_all | solution.py:35
  22.2 17.1 %collective-permute-start.1 = (f32[280,256]{1,0:T(8,128)S(1)}, f32[280,256]{1,0:T(8,128)S(1)}, u32[]{:S(2)}, u32[]{:S(2)}) collective-permute-start(f32[280,256]{1,0:T(8,128)S(1)} %select_maximum_fusion.1), channel_id=1, source_target_pairs={{0,64},{32,96},{64,128},{96,160},{128,192},{160,224},{1,65},{33,97... | collective-permute-start | bytes 860168 | tf_op jit(solution)/shard_map/ppermute | solution.py:18
  33.5 51.3 %all-to-all-start.1 = ((f32[32,8,256]{2,1,0:T(8,128)}), f32[32,8,256]{2,1,0:T(8,128)S(1)}, u32[]{:S(2)}, u32[]{:S(2)}) async-start(f32[32,8,256]{2,1,0:T(8,128)} %gather_fusion), calls=%async_computation.1 | async-start | bytes 524288 | tf_op jit(solution)/shard_map/all_to_all | solution.py:37
  39.9 12.0 %collective-permute-start.2 = (f32[280,256]{1,0:T(8,128)S(1)}, f32[280,256]{1,0:T(8,128)S(1)}, u32[]{:S(2)}, u32[]{:S(2)}) collective-permute-start(f32[280,256]{1,0:T(8,128)S(1)} %select_maximum_fusion), channel_id=1, source_target_pairs={{0,128},{32,160},{64,192},{96,224},{1,129},{33,161},{65,193},{97,2... | collective-permute-start | bytes 860168 | tf_op jit(solution)/shard_map/ppermute | solution.py:18
  69.1 6.9 %copy-start.2 = (f32[1,1,256,256]{3,2,1,0:T(8,128)S(1)}, f32[1,1,256,256]{3,2,1,0:T(8,128)}, u32[]{:S(2)}) copy-start(f32[1,1,256,256]{3,2,1,0:T(8,128)} %param.9) | copy-start | bytes 786436
  69.1 11.4 %slice-start = ((s8[4718592]{0:T(1024)(128)(4,1)}), s8[4194304]{0:T(1024)(128)(4,1)S(1)}, s32[]{:S(2)}) async-start(s8[4718592]{0:T(1024)(128)(4,1)} %bitcast.121), calls=%async_computation.7 | async-start | bytes 8388608
  73.8 2.1 %copy-start.1 = (f32[256,18,256]{2,0,1:T(8,128)}, f32[256,18,256]{2,0,1:T(8,128)S(1)}, u32[]{:S(2)}) copy-start(f32[256,18,256]{2,0,1:T(8,128)S(1)} %fusion.32) | copy-start | bytes 14155780
  76.0 4.5 %slice-start.1 = ((s8[4718592]{0:T(1024)(128)(4,1)}), s8[524288]{0:T(1024)(128)(4,1)S(1)}, s32[]{:S(2)}) async-start(s8[4718592]{0:T(1024)(128)(4,1)} %bitcast.121), calls=%async_computation.8 | async-start | bytes 1048576
  84.8 24.6 %copy-start.3 = (f32[1,1,256,256]{3,2,1,0:T(8,128)S(1)}, f32[1,1,256,256]{3,2,1,0:T(8,128)}, u32[]{:S(2)}) copy-start(f32[1,1,256,256]{3,2,1,0:T(8,128)} %param.15) | copy-start | bytes 786436
  87.7 19.3 %all-to-all-start.2 = ((f32[32,1,2]{2,1,0:T(1,128)}), f32[32,1,2]{2,1,0:T(1,128)S(1)}, u32[]{:S(2)}, u32[]{:S(2)}) async-start(f32[32,1,2]{2,1,0:T(1,128)} %broadcast_in_dim.14), calls=%async_computation.2 | async-start | bytes 32768 | tf_op jit(solution)/shard_map/all_to_all | solution.py:28
  123.9 11.6 %slice-start.2 = ((s8[4718592]{0:T(1024)(128)(4,1)}), s8[524288]{0:T(1024)(128)(4,1)S(1)}, s32[]{:S(2)}) async-start(s8[4718592]{0:T(1024)(128)(4,1)} %bitcast.123), calls=%async_computation.9 | async-start | bytes 1048576
  125.2 15.2 %all-to-all-start.4 = ((f32[32,8,256]{2,1,0:T(8,128)}), f32[32,8,256]{2,1,0:T(8,128)S(1)}, u32[]{:S(2)}, u32[]{:S(2)}) async-start(f32[32,8,256]{2,1,0:T(8,128)} %gather_fusion.1), calls=%async_computation.4 | async-start | bytes 524288 | tf_op jit(solution)/shard_map/all_to_all | solution.py:37
  129.5 6.0 %slice-start.3 = ((s8[4718592]{0:T(1024)(128)(4,1)}), s8[4194304]{0:T(1024)(128)(4,1)S(1)}, s32[]{:S(2)}) async-start(s8[4718592]{0:T(1024)(128)(4,1)} %bitcast.123), calls=%async_computation.10 | async-start | bytes 8388608

commit v3 on v0

--- a/solution.py
+++ b/solution.py
@@ -47,7 +47,7 @@
         out_ref[w] = acc
 
 
-def channel_mix(mix, source, rows=64):
+def channel_mix(mix, source, rows=128):
     channels, height, width = source.shape
     return pl.pallas_call(
         _mix_kernel,

time: 179 us -> 179 us (level)
  no operation moved by 1% of the time
where the time goes in v3:
time: 179 us; the launch traced here: 178 us
  blocking collectives  45.6 us (25%)
  matrix products  39.3 us (22%)
  starting transfers between devices  37.3 us (21%)
  waiting for transfers between devices  23.7 us (13%)
  other arithmetic  10.8 us (6%)
  local copies, waits for them, and re-layouts  9.31 us (5%)
  Pallas kernels  8.57 us (5%)
  between operations  3.63 us (2%)
    all_to_all x2, blocking collectives, sec_total(): return jnp.sum(lax.all_to_all(spread, 'sec', 0, 0, tiled=True), axis=0)  31.5 us
    all_to_all x1, blocking collectives, regroup(): held = lax.all_to_all(pieces, 'sec', 0, 0, tiled=True)  14.1 us
    all_to_all x1, starting transfers between devices, regroup(): held = lax.all_to_all(pieces, 'sec', 0, 0, tiled=True)  11.3 us
    dot_general x2, matrix products, apply_h(): inner = jnp.einsum('iwj,jk->iwk', left_env, vector, precision=HIGH)  10.5 us
    ppermute x3, waiting for transfers between devices, passed_along(): lax.ppermute(value, axis, [(source, source + steps) for source in range(i...  10.1 us
    all_to_all x2, starting transfers between devices, regroup(): back = lax.all_to_all(ordered, 'sec', 0, 0, tiled=True)  10.1 us
    all_to_all x1, starting transfers between devices, sec_total(): return jnp.sum(lax.all_to_all(spread, 'sec', 0, 0, tiled=True), axis=0)  9.5 us
    dot_general x12, matrix products, product(): return jnp.matmul(left, right, precision=HIGH)  9.14 us
  transfers between devices with their start and end apart: 7, of which 4 were waited for; matrix products, arithmetic and copies ran while one was open for 25% of the time, Pallas kernels for 5%

profile of v3, /device:TPU:16, one launch (start us, length us, event | category | flops | bytes accessed | tf_op | source)
XLA Modules:
  0.0 178.2 jit_solution(1994363134102755386)
XLA Ops:
  1.7 1.9 %collective-permute-start = (f32[280,256]{1,0:T(8,128)S(1)}, f32[280,256]{1,0:T(8,128)S(1)}, u32[]{:S(2)}, u32[]{:S(2)}) collective-permute-start(f32[280,256]{1,0:T(8,128)S(1)} %select_maximum_fusion.2), channel_id=1, source_target_pairs={{0,32},{32,64},{64,96},{96,128},{128,160},{160,192},{192,224},{1,3... | collective-permute-start | bytes 860168 | tf_op jit(solution)/shard_map/ppermute | solution.py:18
  3.7 1.4 constant_dynamic-slice_fusion.1
  6.3 2.2 %fusion.19 = f32[32,8,256]{2,1,0:T(8,128)} fusion(f32[1,1,256,256]{3,2,1,0:T(8,128)} %param.15, f32[1,1,256,256]{3,2,1,0:T(8,128)} %param.9, f32[256]{0:T(256)S(1)} %get-tuple-element.23, f32[256]{0:T(256)S(1)} %get-tuple-element.24), kind=kOutput, calls=%fused_computation.34 | convolution fusion | flops 201457664 | bytes 788480 | tf_op jit(solution)/shard_map/dot_general | solution.py:22
  8.5 11.3 %all-to-all-start = ((f32[32,8,256]{2,1,0:T(8,128)}), f32[32,8,256]{2,1,0:T(8,128)S(1)}, u32[]{:S(2)}, u32[]{:S(2)}) async-start(f32[32,8,256]{2,1,0:T(8,128)} %fusion.19), calls=%async_computation | async-start | bytes 524288 | tf_op jit(solution)/shard_map/all_to_all | solution.py:35
  19.8 1.4 convolution_select_fusion.3
  22.2 3.2 %collective-permute-start.1 = (f32[280,256]{1,0:T(8,128)S(1)}, f32[280,256]{1,0:T(8,128)S(1)}, u32[]{:S(2)}, u32[]{:S(2)}) collective-permute-start(f32[280,256]{1,0:T(8,128)S(1)} %select_maximum_fusion.1), channel_id=1, source_target_pairs={{0,64},{32,96},{64,128},{96,160},{128,192},{160,224},{1,65},{33,97... | collective-permute-start | bytes 860168 | tf_op jit(solution)/shard_map/ppermute | solution.py:18
  26.1 6.1 %all-to-all-done = f32[32,8,256]{2,1,0:T(8,128)S(1)} async-done(((f32[32,8,256]{2,1,0:T(8,128)}), f32[32,8,256]{2,1,0:T(8,128)S(1)}, u32[]{:S(2)}, u32[]{:S(2)}) %all-to-all-start) | async-done | bytes 262176 | tf_op jit(solution)/shard_map/all_to_all | solution.py:35
  33.5 5.8 %all-to-all-start.1 = ((f32[32,8,256]{2,1,0:T(8,128)}), f32[32,8,256]{2,1,0:T(8,128)S(1)}, u32[]{:S(2)}, u32[]{:S(2)}) async-start(f32[32,8,256]{2,1,0:T(8,128)} %gather_fusion), calls=%async_computation.1 | async-start | bytes 524288 | tf_op jit(solution)/shard_map/all_to_all | solution.py:37
  41.7 10.1 %collective-permute-done.2 = f32[280,256]{1,0:T(8,128)S(1)} collective-permute-done((f32[280,256]{1,0:T(8,128)S(1)}, f32[280,256]{1,0:T(8,128)S(1)}, u32[]{:S(2)}, u32[]{:S(2)}) %collective-permute-start.2) | collective-permute-done | bytes 286752 | tf_op jit(solution)/shard_map/ppermute | solution.py:18
  52.6 8.6 %shard_map.91 = f32[18,256,256]{2,1,0:T(8,128)} custom-call(f32[18,18]{1,0:T(8,128)} %convolution_select_fusion.4.mix_ref, f32[18,256,256]{2,1,0:T(8,128)} %bitcast.125), custom_call_target="tpu_custom_call" | custom-call | tf_op jit(solution)/shard_map/pallas_call | solution.py:52
  61.5 6.1 %multiply_reduce_fusion = (f32[18,256]{1,0:T(8,128)S(1)}, f32[18,256,256]{2,1,0:T(8,128)S(1)}) fusion(f32[256,256]{1,0:T(8,128)S(1)} %convolution_select_fusion, f32[18,256,256]{2,1,0:T(8,128)} %shard_map.91), kind=kOutput, calls=%fused_computation.8 | convolution fusion | flops 3626233344 | bytes 9717760 | tf_op jit(solution)/shard_map/wkl,lj->wkj/dot_general | solution.py:132
  67.7 4.7 %fusion.32 = f32[256,18,256]{2,0,1:T(8,128)S(1)} fusion(f32[18,256,256]{2,1,0:T(8,128)S(1)} %get-tuple-element.19, f32[256,256]{1,0:T(8,128)S(1)} %convolution_select_fusion), kind=kOutput, calls=%fused_computation.47 | convolution fusion | flops 3623878656 | bytes 9699328 | tf_op jit(solution)/shard_map/ki,wkj->iwj/dot_general | solution.py:133
  72.4 2.1 %copy-done.1 = f32[256,18,256]{2,0,1:T(8,128)} copy-done((f32[256,18,256]{2,0,1:T(8,128)}, f32[256,18,256]{2,0,1:T(8,128)S(1)}, u32[]{:S(2)}) %copy-start.1) | copy-done | bytes 4718616
  74.5 4.5 %fusion.28 = f32[256,18,256]{2,0,1:T(8,128)S(1)} fusion(f32[256,18,256]{2,0,1:T(8,128)S(1)} %fusion.32, f32[1,1,256,256]{3,2,1,0:T(8,128)S(1)} %copy-done.2, f32[256]{0:T(256)S(1)} %get-tuple-element.23, f32[256]{0:T(256)S(1)} %get-tuple-element.24), kind=kOutput, calls=%fused_computation.43 | convolution fusion | flops 3624009728 | bytes 9701376 | tf_op jit(solution)/shard_map/iwj,jk->iwk/dot_general | solution.py:138
  79.1 4.3 %fusion.9 = f32[256,256]{1,0:T(8,128)S(1)} fusion(f32[256,18,256]{2,0,1:T(8,128)S(1)} %fusion.28, f32[1,1,18,256,256]{4,3,2,1,0:T(8,128)S(1)} %bitcast.122), kind=kOutput, calls=%fused_computation.19 | convolution fusion | flops 3623878656 | bytes 9699328 | tf_op jit(solution)/shard_map/iwk,wkl->il/dot_general | solution.py:139
  86.3 9.5 %all-to-all-start.2 = ((f32[32,1,2]{2,1,0:T(1,128)}), f32[32,1,2]{2,1,0:T(1,128)S(1)}, u32[]{:S(2)}, u32[]{:S(2)}) async-start(f32[32,1,2]{2,1,0:T(1,128)} %broadcast_in_dim.14), calls=%async_computation.2 | async-start | bytes 32768 | tf_op jit(solution)/shard_map/all_to_all | solution.py:28
  95.8 3.0 %fusion.4 = f32[18,256]{1,0:T(8,128)S(1)} fusion(f32[1,1,18,256,256]{4,3,2,1,0:T(8,128)} %param.11, f32[256,256]{1,0:T(8,128)S(1)} %fusion.37), kind=kLoop, calls=%fused_computation.7 | loop fusion | flops 2354688 | bytes 4999168 | tf_op jit(solution)/shard_map/reduce_sum | solution.py:129
  98.8 6.7 %all-to-all-done.2 = f32[32,1,2]{2,1,0:T(1,128)S(1)} async-done(((f32[32,1,2]{2,1,0:T(1,128)}), f32[32,1,2]{2,1,0:T(1,128)S(1)}, u32[]{:S(2)}, u32[]{:S(2)}) %all-to-all-start.2) | async-done | bytes 288 | tf_op jit(solution)/shard_map/all_to_all | solution.py:28
  108.3 14.1 %all_to_all.38 = f32[32,8,256]{2,1,0:T(8,128)S(1)} all-to-all(f32[32,8,256]{2,1,0:T(8,128)S(1)} %fusion.17), channel_id=1, replica_groups=mesh['seg'=8,'sec'=32] {'sec'}, dimensions={0} | all-to-all | bytes 524288 | tf_op jit(solution)/shard_map/all_to_all | solution.py:35
  123.7 4.3 %all-to-all-start.4 = ((f32[32,8,256]{2,1,0:T(8,128)}), f32[32,8,256]{2,1,0:T(8,128)S(1)}, u32[]{:S(2)}, u32[]{:S(2)}) async-start(f32[32,8,256]{2,1,0:T(8,128)} %gather_fusion.1), calls=%async_computation.4 | async-start | bytes 524288 | tf_op jit(solution)/shard_map/all_to_all | solution.py:37
  128.0 6.0 %fusion.22 = f32[256,18,256]{2,0,1:T(8,128)S(1)} fusion(f32[256,18,256]{2,0,1:T(8,128)} %copy-done.1, f32[256,256]{1,0:T(8,128)S(1)} %get-tuple-element.20), kind=kOutput, calls=%fused_computation.37 | convolution fusion | flops 3623878656 | bytes 9699328 | tf_op jit(solution)/shard_map/iwj,jk->iwk/dot_general | solution.py:138
  134.1 4.1 %fusion.12 = f32[256,256]{1,0:T(8,128)S(1)} fusion(f32[256,18,256]{2,0,1:T(8,128)S(1)} %fusion.22, f32[1,1,18,256,256]{4,3,2,1,0:T(8,128)S(1)} %bitcast.124), kind=kOutput, calls=%fused_computation.20 | convolution fusion | flops 3623878656 | bytes 9699328 | tf_op jit(solution)/shard_map/iwk,wkl->il/dot_general | solution.py:139
  141.3 18.7 %all_to_all.39 = f32[32,1,2]{2,1,0:T(1,128)S(1)} all-to-all(f32[32,1,2]{2,1,0:T(1,128)S(1)} %broadcast_in_dim.15), channel_id=1, replica_groups=mesh['seg'=8,'sec'=32] {'sec'}, dimensions={0} | all-to-all | bytes 512 | tf_op jit(solution)/shard_map/all_to_all | solution.py:28
  163.4 12.8 %all_to_all.40 = f32[32,1,1]{2,1,0:T(1,128)S(1)} all-to-all(f32[32,1,1]{2,1,0:T(1,128)S(1)} %broadcast_in_dim.16), channel_id=1, replica_groups=mesh['seg'=8,'sec'=32] {'sec'}, dimensions={0} | all-to-all | bytes 256 | tf_op jit(solution)/shard_map/all_to_all | solution.py:28
  (54 shorter events, 21.7 us)
Async XLA Ops:
  0.0 83.4 %copy-start = (f32[1,1,256,256]{3,2,1,0:T(8,128)S(1)}, f32[1,1,256,256]{3,2,1,0:T(8,128)}, u32[]{:S(2)}) copy-start(f32[1,1,256,256]{3,2,1,0:T(8,128)} %param.14) | copy-start | bytes 786436
  1.7 18.1 %collective-permute-start = (f32[280,256]{1,0:T(8,128)S(1)}, f32[280,256]{1,0:T(8,128)S(1)}, u32[]{:S(2)}, u32[]{:S(2)}) collective-permute-start(f32[280,256]{1,0:T(8,128)S(1)} %select_maximum_fusion.2), channel_id=1, source_target_pairs={{0,32},{32,64},{64,96},{96,128},{128,160},{160,192},{192,224},{1,3... | collective-permute-start | bytes 860168 | tf_op jit(solution)/shard_map/ppermute | solution.py:18
  8.5 23.7 %all-to-all-start = ((f32[32,8,256]{2,1,0:T(8,128)}), f32[32,8,256]{2,1,0:T(8,128)S(1)}, u32[]{:S(2)}, u32[]{:S(2)}) async-start(f32[32,8,256]{2,1,0:T(8,128)} %fusion.19), calls=%async_computation | async-start | bytes 524288 | tf_op jit(solution)/shard_map/all_to_all | solution.py:35
  22.2 17.1 %collective-permute-start.1 = (f32[280,256]{1,0:T(8,128)S(1)}, f32[280,256]{1,0:T(8,128)S(1)}, u32[]{:S(2)}, u32[]{:S(2)}) collective-permute-start(f32[280,256]{1,0:T(8,128)S(1)} %select_maximum_fusion.1), channel_id=1, source_target_pairs={{0,64},{32,96},{64,128},{96,160},{128,192},{160,224},{1,65},{33,97... | collective-permute-start | bytes 860168 | tf_op jit(solution)/shard_map/ppermute | solution.py:18
  33.5 49.8 %all-to-all-start.1 = ((f32[32,8,256]{2,1,0:T(8,128)}), f32[32,8,256]{2,1,0:T(8,128)S(1)}, u32[]{:S(2)}, u32[]{:S(2)}) async-start(f32[32,8,256]{2,1,0:T(8,128)} %gather_fusion), calls=%async_computation.1 | async-start | bytes 524288 | tf_op jit(solution)/shard_map/all_to_all | solution.py:37
  39.9 12.0 %collective-permute-start.2 = (f32[280,256]{1,0:T(8,128)S(1)}, f32[280,256]{1,0:T(8,128)S(1)}, u32[]{:S(2)}, u32[]{:S(2)}) collective-permute-start(f32[280,256]{1,0:T(8,128)S(1)} %select_maximum_fusion), channel_id=1, source_target_pairs={{0,128},{32,160},{64,192},{96,224},{1,129},{33,161},{65,193},{97,2... | collective-permute-start | bytes 860168 | tf_op jit(solution)/shard_map/ppermute | solution.py:18
  67.6 6.9 %copy-start.2 = (f32[1,1,256,256]{3,2,1,0:T(8,128)S(1)}, f32[1,1,256,256]{3,2,1,0:T(8,128)}, u32[]{:S(2)}) copy-start(f32[1,1,256,256]{3,2,1,0:T(8,128)} %param.9) | copy-start | bytes 786436
  67.6 11.4 %slice-start = ((s8[4718592]{0:T(1024)(128)(4,1)}), s8[4194304]{0:T(1024)(128)(4,1)S(1)}, s32[]{:S(2)}) async-start(s8[4718592]{0:T(1024)(128)(4,1)} %bitcast.121), calls=%async_computation.7 | async-start | bytes 8388608
  72.4 2.1 %copy-start.1 = (f32[256,18,256]{2,0,1:T(8,128)}, f32[256,18,256]{2,0,1:T(8,128)S(1)}, u32[]{:S(2)}) copy-start(f32[256,18,256]{2,0,1:T(8,128)S(1)} %fusion.32) | copy-start | bytes 14155780
  74.5 4.5 %slice-start.1 = ((s8[4718592]{0:T(1024)(128)(4,1)}), s8[524288]{0:T(1024)(128)(4,1)S(1)}, s32[]{:S(2)}) async-start(s8[4718592]{0:T(1024)(128)(4,1)} %bitcast.121), calls=%async_computation.8 | async-start | bytes 1048576
  83.3 24.5 %copy-start.3 = (f32[1,1,256,256]{3,2,1,0:T(8,128)S(1)}, f32[1,1,256,256]{3,2,1,0:T(8,128)}, u32[]{:S(2)}) copy-start(f32[1,1,256,256]{3,2,1,0:T(8,128)} %param.15) | copy-start | bytes 786436
  86.3 19.2 %all-to-all-start.2 = ((f32[32,1,2]{2,1,0:T(1,128)}), f32[32,1,2]{2,1,0:T(1,128)S(1)}, u32[]{:S(2)}, u32[]{:S(2)}) async-start(f32[32,1,2]{2,1,0:T(1,128)} %broadcast_in_dim.14), calls=%async_computation.2 | async-start | bytes 32768 | tf_op jit(solution)/shard_map/all_to_all | solution.py:28
  122.4 11.6 %slice-start.2 = ((s8[4718592]{0:T(1024)(128)(4,1)}), s8[524288]{0:T(1024)(128)(4,1)S(1)}, s32[]{:S(2)}) async-start(s8[4718592]{0:T(1024)(128)(4,1)} %bitcast.123), calls=%async_computation.9 | async-start | bytes 1048576
  123.7 15.2 %all-to-all-start.4 = ((f32[32,8,256]{2,1,0:T(8,128)}), f32[32,8,256]{2,1,0:T(8,128)S(1)}, u32[]{:S(2)}, u32[]{:S(2)}) async-start(f32[32,8,256]{2,1,0:T(8,128)} %gather_fusion.1), calls=%async_computation.4 | async-start | bytes 524288 | tf_op jit(solution)/shard_map/all_to_all | solution.py:37
  128.0 6.0 %slice-start.3 = ((s8[4718592]{0:T(1024)(128)(4,1)}), s8[4194304]{0:T(1024)(128)(4,1)S(1)}, s32[]{:S(2)}) async-start(s8[4718592]{0:T(1024)(128)(4,1)} %bitcast.123), calls=%async_computation.10 | async-start | bytes 8388608

commit v4 on v0

--- a/solution.py
+++ b/solution.py
@@ -33,7 +33,8 @@
     rows, cols = moving.shape
     pieces = moving.reshape(count, rows // count, cols)
     held = lax.all_to_all(pieces, "sec", 0, 0, tiled=True)
-    ordered = jnp.take(held, wanted, axis=0, mode="clip")
+    chooser = (wanted[:, None] == lax.broadcasted_iota(jnp.int32, (1, count), 1)).astype(held.dtype)
+    ordered = jnp.einsum("bc,cpq->bpq", chooser, held, precision=HIGH)
     back = lax.all_to_all(ordered, "sec", 0, 0, tiled=True)
     return back.reshape(rows, cols)
 

time: 179 us -> 180 us (level)
    gather x2 -> x0, local copies, waits for them, and re-layouts: 2.57 us -> none  [regroup(): ordered = jnp.take(held, wanted, axis=0, mode='clip')]
where the time goes in v4:
time: 180 us; the launch traced here: 179 us
  blocking collectives  45.6 us (25%)
  matrix products  40.6 us (23%)
  starting transfers between devices  37.3 us (21%)
  waiting for transfers between devices  24.3 us (14%)
  other arithmetic  10.2 us (6%)
  local copies, waits for them, and re-layouts  8.49 us (5%)
  Pallas kernels  8.32 us (5%)
  between operations  3.75 us (2%)
    all_to_all x2, blocking collectives, sec_total(): return jnp.sum(lax.all_to_all(spread, 'sec', 0, 0, tiled=True), axis=0)  31.5 us
    all_to_all x1, blocking collectives, regroup(): held = lax.all_to_all(pieces, 'sec', 0, 0, tiled=True)  14.1 us
    all_to_all x1, starting transfers between devices, regroup(): held = lax.all_to_all(pieces, 'sec', 0, 0, tiled=True)  11.3 us
    dot_general x2, matrix products, apply_h(): inner = jnp.einsum('iwj,jk->iwk', left_env, vector, precision=HIGH)  10.5 us
    ppermute x3, waiting for transfers between devices, passed_along(): lax.ppermute(value, axis, [(source, source + steps) for source in range(i...  10.1 us
    all_to_all x2, starting transfers between devices, regroup(): back = lax.all_to_all(ordered, 'sec', 0, 0, tiled=True)  10.1 us
    all_to_all x1, starting transfers between devices, sec_total(): return jnp.sum(lax.all_to_all(spread, 'sec', 0, 0, tiled=True), axis=0)  9.51 us
    dot_general x12, matrix products, product(): return jnp.matmul(left, right, precision=HIGH)  9.15 us
  transfers between devices with their start and end apart: 7, of which 4 were waited for; matrix products, arithmetic and copies ran while one was open for 25% of the time, Pallas kernels for 5%

profile of v4, /device:TPU:16, one launch (start us, length us, event | category | flops | bytes accessed | tf_op | source)
XLA Modules:
  0.0 178.6 jit_solution(12471762722366106116)
XLA Ops:
  1.7 1.9 %collective-permute-start = (f32[280,256]{1,0:T(8,128)S(1)}, f32[280,256]{1,0:T(8,128)S(1)}, u32[]{:S(2)}, u32[]{:S(2)}) collective-permute-start(f32[280,256]{1,0:T(8,128)S(1)} %select_maximum_fusion.2), channel_id=1, source_target_pairs={{0,32},{32,64},{64,96},{96,128},{128,160},{160,192},{192,224},{1,3... | collective-permute-start | bytes 860168 | tf_op jit(solution)/shard_map/ppermute | solution.py:18
  3.7 1.4 constant_dynamic-slice_fusion.1
  6.3 2.1 %fusion.19 = f32[32,8,256]{2,1,0:T(8,128)} fusion(f32[1,1,256,256]{3,2,1,0:T(8,128)} %param.15, f32[1,1,256,256]{3,2,1,0:T(8,128)} %param.9, f32[256]{0:T(256)S(1)} %get-tuple-element.23, f32[256]{0:T(256)S(1)} %get-tuple-element.24), kind=kOutput, calls=%fused_computation.32 | convolution fusion | flops 201457664 | bytes 788480 | tf_op jit(solution)/shard_map/dot_general | solution.py:22
  8.4 11.3 %all-to-all-start = ((f32[32,8,256]{2,1,0:T(8,128)}), f32[32,8,256]{2,1,0:T(8,128)S(1)}, u32[]{:S(2)}, u32[]{:S(2)}) async-start(f32[32,8,256]{2,1,0:T(8,128)} %fusion.19), calls=%async_computation | async-start | bytes 524288 | tf_op jit(solution)/shard_map/all_to_all | solution.py:35
  20.7 1.4 convolution_select_fusion.3
  22.2 3.2 %collective-permute-start.1 = (f32[280,256]{1,0:T(8,128)S(1)}, f32[280,256]{1,0:T(8,128)S(1)}, u32[]{:S(2)}, u32[]{:S(2)}) collective-permute-start(f32[280,256]{1,0:T(8,128)S(1)} %select_maximum_fusion.1), channel_id=1, source_target_pairs={{0,64},{32,96},{64,128},{96,160},{128,192},{160,224},{1,65},{33,97... | collective-permute-start | bytes 860168 | tf_op jit(solution)/shard_map/ppermute | solution.py:18
  25.4 6.8 %all-to-all-done = f32[32,8,256]{2,1,0:T(8,128)S(1)} async-done(((f32[32,8,256]{2,1,0:T(8,128)}), f32[32,8,256]{2,1,0:T(8,128)S(1)}, u32[]{:S(2)}, u32[]{:S(2)}) %all-to-all-start) | async-done | bytes 262176 | tf_op jit(solution)/shard_map/all_to_all | solution.py:35
  34.0 5.8 %all-to-all-start.1 = ((f32[32,8,256]{2,1,0:T(8,128)}), f32[32,8,256]{2,1,0:T(8,128)S(1)}, u32[]{:S(2)}, u32[]{:S(2)}) async-start(f32[32,8,256]{2,1,0:T(8,128)} %copy.40), calls=%async_computation.1 | async-start | bytes 524288 | tf_op jit(solution)/shard_map/all_to_all | solution.py:38
  42.2 10.1 %collective-permute-done.2 = f32[280,256]{1,0:T(8,128)S(1)} collective-permute-done((f32[280,256]{1,0:T(8,128)S(1)}, f32[280,256]{1,0:T(8,128)S(1)}, u32[]{:S(2)}, u32[]{:S(2)}) %collective-permute-start.2) | collective-permute-done | bytes 286752 | tf_op jit(solution)/shard_map/ppermute | solution.py:18
  53.1 8.3 %shard_map.91 = f32[18,256,256]{2,1,0:T(8,128)} custom-call(f32[18,18]{1,0:T(8,128)} %convolution_select_fusion.4.mix_ref, f32[18,256,256]{2,1,0:T(8,128)} %bitcast.129), custom_call_target="tpu_custom_call" | custom-call | tf_op jit(solution)/shard_map/pallas_call | solution.py:53
  61.8 6.1 %multiply_reduce_fusion = (f32[18,256]{1,0:T(8,128)S(1)}, f32[18,256,256]{2,1,0:T(8,128)S(1)}) fusion(f32[256,256]{1,0:T(8,128)S(1)} %convolution_select_fusion, f32[18,256,256]{2,1,0:T(8,128)} %shard_map.91), kind=kOutput, calls=%fused_computation.6 | convolution fusion | flops 3626233344 | bytes 9717760 | tf_op jit(solution)/shard_map/wkl,lj->wkj/dot_general | solution.py:133
  67.9 4.7 %fusion.32 = f32[256,18,256]{2,0,1:T(8,128)S(1)} fusion(f32[18,256,256]{2,1,0:T(8,128)S(1)} %get-tuple-element.19, f32[256,256]{1,0:T(8,128)S(1)} %convolution_select_fusion), kind=kOutput, calls=%fused_computation.45 | convolution fusion | flops 3623878656 | bytes 9699328 | tf_op jit(solution)/shard_map/ki,wkj->iwj/dot_general | solution.py:134
  72.7 2.1 %copy-done.1 = f32[256,18,256]{2,0,1:T(8,128)} copy-done((f32[256,18,256]{2,0,1:T(8,128)}, f32[256,18,256]{2,0,1:T(8,128)S(1)}, u32[]{:S(2)}) %copy-start.1) | copy-done | bytes 4718616
  74.8 4.5 %fusion.28 = f32[256,18,256]{2,0,1:T(8,128)S(1)} fusion(f32[256,18,256]{2,0,1:T(8,128)S(1)} %fusion.32, f32[1,1,256,256]{3,2,1,0:T(8,128)S(1)} %copy-done.2, f32[256]{0:T(256)S(1)} %get-tuple-element.23, f32[256]{0:T(256)S(1)} %get-tuple-element.24), kind=kOutput, calls=%fused_computation.41 | convolution fusion | flops 3624009728 | bytes 9701376 | tf_op jit(solution)/shard_map/iwj,jk->iwk/dot_general | solution.py:139
  79.3 4.3 %fusion.9 = f32[256,256]{1,0:T(8,128)S(1)} fusion(f32[256,18,256]{2,0,1:T(8,128)S(1)} %fusion.28, f32[1,1,18,256,256]{4,3,2,1,0:T(8,128)S(1)} %bitcast.126), kind=kOutput, calls=%fused_computation.17 | convolution fusion | flops 3623878656 | bytes 9699328 | tf_op jit(solution)/shard_map/iwk,wkl->il/dot_general | solution.py:140
  86.7 9.5 %all-to-all-start.2 = ((f32[32,1,2]{2,1,0:T(1,128)}), f32[32,1,2]{2,1,0:T(1,128)S(1)}, u32[]{:S(2)}, u32[]{:S(2)}) async-start(f32[32,1,2]{2,1,0:T(1,128)} %broadcast_in_dim.8), calls=%async_computation.2 | async-start | bytes 32768 | tf_op jit(solution)/shard_map/all_to_all | solution.py:28
  96.2 3.0 %fusion.4 = f32[18,256]{1,0:T(8,128)S(1)} fusion(f32[1,1,18,256,256]{4,3,2,1,0:T(8,128)} %param.11, f32[256,256]{1,0:T(8,128)S(1)} %fusion.41), kind=kLoop, calls=%fused_computation.5 | loop fusion | flops 2354688 | bytes 4999168 | tf_op jit(solution)/shard_map/reduce_sum | solution.py:130
  99.2 6.7 %all-to-all-done.2 = f32[32,1,2]{2,1,0:T(1,128)S(1)} async-done(((f32[32,1,2]{2,1,0:T(1,128)}), f32[32,1,2]{2,1,0:T(1,128)S(1)}, u32[]{:S(2)}, u32[]{:S(2)}) %all-to-all-start.2) | async-done | bytes 288 | tf_op jit(solution)/shard_map/all_to_all | solution.py:28
  108.8 14.1 %all_to_all.38 = f32[32,8,256]{2,1,0:T(8,128)S(1)} all-to-all(f32[32,8,256]{2,1,0:T(8,128)S(1)} %fusion.17), channel_id=1, replica_groups=mesh['seg'=8,'sec'=32] {'sec'}, dimensions={0} | all-to-all | bytes 524288 | tf_op jit(solution)/shard_map/all_to_all | solution.py:35
  124.2 4.3 %all-to-all-start.4 = ((f32[32,8,256]{2,1,0:T(8,128)}), f32[32,8,256]{2,1,0:T(8,128)S(1)}, u32[]{:S(2)}, u32[]{:S(2)}) async-start(f32[32,8,256]{2,1,0:T(8,128)} %copy.45), calls=%async_computation.4 | async-start | bytes 524288 | tf_op jit(solution)/shard_map/all_to_all | solution.py:38
  128.5 6.0 %fusion.22 = f32[256,18,256]{2,0,1:T(8,128)S(1)} fusion(f32[256,18,256]{2,0,1:T(8,128)} %copy-done.1, f32[256,256]{1,0:T(8,128)S(1)} %get-tuple-element.20), kind=kOutput, calls=%fused_computation.35 | convolution fusion | flops 3623878656 | bytes 9699328 | tf_op jit(solution)/shard_map/iwj,jk->iwk/dot_general | solution.py:139
  134.5 4.1 %fusion.12 = f32[256,256]{1,0:T(8,128)S(1)} fusion(f32[256,18,256]{2,0,1:T(8,128)S(1)} %fusion.22, f32[1,1,18,256,256]{4,3,2,1,0:T(8,128)S(1)} %bitcast.128), kind=kOutput, calls=%fused_computation.18 | convolution fusion | flops 3623878656 | bytes 9699328 | tf_op jit(solution)/shard_map/iwk,wkl->il/dot_general | solution.py:140
  141.7 18.7 %all_to_all.39 = f32[32,1,2]{2,1,0:T(1,128)S(1)} all-to-all(f32[32,1,2]{2,1,0:T(1,128)S(1)} %broadcast_in_dim.9), channel_id=1, replica_groups=mesh['seg'=8,'sec'=32] {'sec'}, dimensions={0} | all-to-all | bytes 512 | tf_op jit(solution)/shard_map/all_to_all | solution.py:28
  163.7 12.8 %all_to_all.40 = f32[32,1,1]{2,1,0:T(1,128)S(1)} all-to-all(f32[32,1,1]{2,1,0:T(1,128)S(1)} %broadcast_in_dim.10), channel_id=1, replica_groups=mesh['seg'=8,'sec'=32] {'sec'}, dimensions={0} | all-to-all | bytes 256 | tf_op jit(solution)/shard_map/all_to_all | solution.py:28
  (57 shorter events, 21.5 us)
Async XLA Ops:
  0.0 83.6 %copy-start = (f32[1,1,256,256]{3,2,1,0:T(8,128)S(1)}, f32[1,1,256,256]{3,2,1,0:T(8,128)}, u32[]{:S(2)}) copy-start(f32[1,1,256,256]{3,2,1,0:T(8,128)} %param.14) | copy-start | bytes 786436
  1.7 18.1 %collective-permute-start = (f32[280,256]{1,0:T(8,128)S(1)}, f32[280,256]{1,0:T(8,128)S(1)}, u32[]{:S(2)}, u32[]{:S(2)}) collective-permute-start(f32[280,256]{1,0:T(8,128)S(1)} %select_maximum_fusion.2), channel_id=1, source_target_pairs={{0,32},{32,64},{64,96},{96,128},{128,160},{160,192},{192,224},{1,3... | collective-permute-start | bytes 860168 | tf_op jit(solution)/shard_map/ppermute | solution.py:18
  8.4 23.7 %all-to-all-start = ((f32[32,8,256]{2,1,0:T(8,128)}), f32[32,8,256]{2,1,0:T(8,128)S(1)}, u32[]{:S(2)}, u32[]{:S(2)}) async-start(f32[32,8,256]{2,1,0:T(8,128)} %fusion.19), calls=%async_computation | async-start | bytes 524288 | tf_op jit(solution)/shard_map/all_to_all | solution.py:35
  22.2 17.6 %collective-permute-start.1 = (f32[280,256]{1,0:T(8,128)S(1)}, f32[280,256]{1,0:T(8,128)S(1)}, u32[]{:S(2)}, u32[]{:S(2)}) collective-permute-start(f32[280,256]{1,0:T(8,128)S(1)} %select_maximum_fusion.1), channel_id=1, source_target_pairs={{0,64},{32,96},{64,128},{96,160},{128,192},{160,224},{1,65},{33,97... | collective-permute-start | bytes 860168 | tf_op jit(solution)/shard_map/ppermute | solution.py:18
  34.0 49.6 %all-to-all-start.1 = ((f32[32,8,256]{2,1,0:T(8,128)}), f32[32,8,256]{2,1,0:T(8,128)S(1)}, u32[]{:S(2)}, u32[]{:S(2)}) async-start(f32[32,8,256]{2,1,0:T(8,128)} %copy.40), calls=%async_computation.1 | async-start | bytes 524288 | tf_op jit(solution)/shard_map/all_to_all | solution.py:38
  40.4 12.0 %collective-permute-start.2 = (f32[280,256]{1,0:T(8,128)S(1)}, f32[280,256]{1,0:T(8,128)S(1)}, u32[]{:S(2)}, u32[]{:S(2)}) collective-permute-start(f32[280,256]{1,0:T(8,128)S(1)} %select_maximum_fusion), channel_id=1, source_target_pairs={{0,128},{32,160},{64,192},{96,224},{1,129},{33,161},{65,193},{97,2... | collective-permute-start | bytes 860168 | tf_op jit(solution)/shard_map/ppermute | solution.py:18
  67.9 6.9 %copy-start.2 = (f32[1,1,256,256]{3,2,1,0:T(8,128)S(1)}, f32[1,1,256,256]{3,2,1,0:T(8,128)}, u32[]{:S(2)}) copy-start(f32[1,1,256,256]{3,2,1,0:T(8,128)} %param.9) | copy-start | bytes 786436
  67.9 11.4 %slice-start = ((s8[4718592]{0:T(1024)(128)(4,1)}), s8[4194304]{0:T(1024)(128)(4,1)S(1)}, s32[]{:S(2)}) async-start(s8[4718592]{0:T(1024)(128)(4,1)} %bitcast.125), calls=%async_computation.7 | async-start | bytes 8388608
  72.6 2.1 %copy-start.1 = (f32[256,18,256]{2,0,1:T(8,128)}, f32[256,18,256]{2,0,1:T(8,128)S(1)}, u32[]{:S(2)}) copy-start(f32[256,18,256]{2,0,1:T(8,128)S(1)} %fusion.32) | copy-start | bytes 14155780
  74.8 4.5 %slice-start.1 = ((s8[4718592]{0:T(1024)(128)(4,1)}), s8[524288]{0:T(1024)(128)(4,1)S(1)}, s32[]{:S(2)}) async-start(s8[4718592]{0:T(1024)(128)(4,1)} %bitcast.125), calls=%async_computation.8 | async-start | bytes 1048576
  83.6 24.8 %copy-start.3 = (f32[1,1,256,256]{3,2,1,0:T(8,128)S(1)}, f32[1,1,256,256]{3,2,1,0:T(8,128)}, u32[]{:S(2)}) copy-start(f32[1,1,256,256]{3,2,1,0:T(8,128)} %param.15) | copy-start | bytes 786436
  83.6 39.3 %copy-start.4 = (s32[1,32]{1,0:T(1,128)S(1)}, s32[1,32]{1,0:T(1,128)}, u32[]{:S(2)}) copy-start(s32[1,32]{1,0:T(1,128)} %param.17) | copy-start | bytes 388
  86.7 19.3 %all-to-all-start.2 = ((f32[32,1,2]{2,1,0:T(1,128)}), f32[32,1,2]{2,1,0:T(1,128)S(1)}, u32[]{:S(2)}, u32[]{:S(2)}) async-start(f32[32,1,2]{2,1,0:T(1,128)} %broadcast_in_dim.8), calls=%async_computation.2 | async-start | bytes 32768 | tf_op jit(solution)/shard_map/all_to_all | solution.py:28
  123.3 11.2 %slice-start.2 = ((s8[4718592]{0:T(1024)(128)(4,1)}), s8[524288]{0:T(1024)(128)(4,1)S(1)}, s32[]{:S(2)}) async-start(s8[4718592]{0:T(1024)(128)(4,1)} %bitcast.127), calls=%async_computation.9 | async-start | bytes 1048576
  124.2 15.2 %all-to-all-start.4 = ((f32[32,8,256]{2,1,0:T(8,128)}), f32[32,8,256]{2,1,0:T(8,128)S(1)}, u32[]{:S(2)}, u32[]{:S(2)}) async-start(f32[32,8,256]{2,1,0:T(8,128)} %copy.45), calls=%async_computation.4 | async-start | bytes 524288 | tf_op jit(solution)/shard_map/all_to_all | solution.py:38
  128.5 6.0 %slice-start.3 = ((s8[4718592]{0:T(1024)(128)(4,1)}), s8[4194304]{0:T(1024)(128)(4,1)S(1)}, s32[]{:S(2)}) async-start(s8[4718592]{0:T(1024)(128)(4,1)} %bitcast.127), calls=%async_computation.10 | async-start | bytes 8388608
